TPU v7x, 128 devices: a whole 4x4x4 slice. The times are simulated.
128 devices in a mesh: rad: 8 (over x, z_lo), azi: 16 (over z_hi, y, core).
Axes of the slice: x: 4, y: 4, z: 4 (z_hi: 2, z_lo: 2; z = z_hi * 2 + z_lo), core: 2. Of those that a mesh axis runs over, the one named last changes fastest.
Arguments:
- fluid_state: float32 [64, 8, 16, 16384], P('rad', None, None, 'azi'), may hold values from -6 to 6
- orbit_shift: int32 [64], P('rad'), may hold values from 0 to 16383
- residual_speed: float32 [64], P('rad'), may hold values from -0.5 to 0.5
- coupling: float32 [8, 8], replicated, may hold values from -1.2 to 1.2
- radial_solve: float32 [8, 64, 64], replicated, as said below
Outputs:
- advanced: float32 [64, 8, 16, 16384], P('rad', None, None, 'azi')
Inputs may be any that keep to these rules, and one draw needn't show every extreme that they name: radial_solve is, for each field, a dense block of the inverse of the radial operator over the window's radii, whose entries fall off with the distance of the two radii.
All inputs are finite; a program needn't handle non-finite values.
Results may differ from a plain program's by a relative error of at most 0.0003.
Values sent between devices are 32-bit elements; how exact they have to be, the bound alone decides.
No kernel may reach another device: no remote copies, remote signals or barrier semaphores. Data moves between devices by JAX's collectives and lax.ppermute only.
A program may use at most 128 MiB of HBM per device.

v0:
```python
import jax
import jax.numpy as jnp
from jax import lax
from jax.sharding import PartitionSpec as P


def with_halo(cells, sides, width, closed):
    for axis, dim in sides:
        count = lax.axis_size(axis)
        ends = count if closed else count - 1
        head = lax.slice_in_dim(cells, 0, width, axis=dim)
        tail = lax.slice_in_dim(cells, cells.shape[dim] - width, cells.shape[dim], axis=dim)
        cells = jnp.concatenate(
            [
                lax.ppermute(tail, axis, [(i, (i + 1) % count) for i in range(ends)]),
                cells,
                lax.ppermute(head, axis, [((i + 1) % count, i) for i in range(ends)]),
            ],
            axis=dim,
        )
    return cells


def from_behind(value, axis, steps):
    count = lax.axis_size(axis)
    pairs = [(source, (source + steps) % count) for source in range(count)]
    return lax.ppermute(value, axis, pairs)


def face_flux(left, right, speed):
    return 0.5 * speed * (left + right) - 0.5 * jnp.abs(speed) * (right - left)


def radial_term(advected, padded, coupling):
    return advected + jnp.einsum(
        "fg,rgzj->rfzj", coupling, padded[2:] - padded[:-2], precision=lax.Precision.HIGHEST
    )


def implicit_step(radial_solve, explicit):
    return jnp.einsum("frk,kfzj->rfzj", radial_solve, explicit, precision=lax.Precision.HIGHEST)


def band_rim(advected, coupling):
    padded = with_halo(advected, (("rad", 0),), 1, False)
    return radial_term(advected, padded, coupling)


def per_device(fluid_state, orbit_shift, residual_speed, coupling, radial_solve):
    rows, fields, planes, cells = fluid_state.shape
    blocks = lax.axis_size("azi")
    turns = orbit_shift // cells
    rest = orbit_shift % cells
    current = fluid_state
    power = 1
    while power < blocks:
        moved = from_behind(current, "azi", power)
        taken = turns // power % 2 == 1
        current = jnp.where(taken[:, None, None, None], moved, current)
        power = power * 2
    before = from_behind(current, "azi", 1)
    joined = jnp.concatenate([before, current], axis=3)

    def pick_row(row, start):
        return lax.dynamic_slice_in_dim(row, start, cells, axis=2)

    remapped = jax.vmap(pick_row)(joined, cells - rest)
    rimmed = with_halo(remapped, (("azi", 3),), 1, True)
    speed = residual_speed[:, None, None, None]
    lower = rimmed[:, :, :, :-2]
    upper = rimmed[:, :, :, 2:]
    advected = remapped - (face_flux(remapped, upper, speed) - face_flux(lower, remapped, speed))
    explicit = band_rim(advected, coupling)
    return lax.all_to_all(
        implicit_step(
            radial_solve, lax.all_to_all(explicit, "rad", split_axis=3, concat_axis=0, tiled=True)
        ),
        "rad",
        split_axis=0,
        concat_axis=3,
        tiled=True,
    )


def solution(mesh):
    return jax.shard_map(
        per_device,
        mesh=mesh,
        in_specs=(P("rad", None, None, "azi"), P("rad"), P("rad"), P(), P()),
        out_specs=P("rad", None, None, "azi"),
        check_vma=False,
    )
```

profile of v0, /device:TPU:16, one launch (start us, length us, event | category | flops | bytes accessed | tf_op | source)
XLA Modules:
  0.0 700.2 jit_solution(4676089002944819652)
XLA Ops:
  0.8 47.4 %collective-permute-done = f32[8,8,16,1024]{3,2,1,0:T(8,128)S(1)} collective-permute-done((f32[8,8,16,1024]{3,2,1,0:T(8,128)}, f32[8,8,16,1024]{3,2,1,0:T(8,128)S(1)}, u32[]{:S(2)}, u32[]{:S(2)}) %collective-permute-start) | collective-permute-done | bytes 4194336 | tf_op jit(solution)/shard_map/ppermute | solution.py:27
  48.1 3.2 broadcast_select_fusion
  51.3 1.4 collective-permute-start.1
  52.7 90.7 %collective-permute-done.1 = f32[8,8,16,1024]{3,2,1,0:T(8,128)S(1)} collective-permute-done((f32[8,8,16,1024]{3,2,1,0:T(8,128)S(1)}, f32[8,8,16,1024]{3,2,1,0:T(8,128)S(1)}, u32[]{:S(2)}, u32[]{:S(2)}) %collective-permute-start.1) | collective-permute-done | bytes 4194336 | tf_op jit(solution)/shard_map/ppermute | solution.py:27
  143.3 1.4 broadcast_select_fusion.1
  144.8 7.2 %collective-permute-start.2 = (f32[8,8,16,1024]{3,2,1,0:T(8,128)S(1)}, f32[8,8,16,1024]{3,2,1,0:T(8,128)S(1)}, u32[]{:S(2)}, u32[]{:S(2)}) collective-permute-start(f32[8,8,16,1024]{3,2,1,0:T(8,128)S(1)} %broadcast_select_fusion.1), channel_id=1, source_target_pairs={{0,4},{1,5},{2,6},{3,7},{4,8},{5,9},{6,10},{7,11},{8,12},{9,13},{1... | collective-permute-start | bytes 12582920 | tf_op jit(solution)/shard_map/ppermute | solution.py:27
  151.9 87.3 %collective-permute-done.2 = f32[8,8,16,1024]{3,2,1,0:T(8,128)S(1)} collective-permute-done((f32[8,8,16,1024]{3,2,1,0:T(8,128)S(1)}, f32[8,8,16,1024]{3,2,1,0:T(8,128)S(1)}, u32[]{:S(2)}, u32[]{:S(2)}) %collective-permute-start.2) | collective-permute-done | bytes 4194336 | tf_op jit(solution)/shard_map/ppermute | solution.py:27
  239.2 1.4 broadcast_select_fusion.2
  240.7 1.3 collective-permute-start.3
  241.9 92.1 %collective-permute-done.3 = f32[8,8,16,1024]{3,2,1,0:T(8,128)S(1)} collective-permute-done((f32[8,8,16,1024]{3,2,1,0:T(8,128)S(1)}, f32[8,8,16,1024]{3,2,1,0:T(8,128)S(1)}, u32[]{:S(2)}, u32[]{:S(2)}) %collective-permute-start.3) | collective-permute-done | bytes 4194336 | tf_op jit(solution)/shard_map/ppermute | solution.py:27
  334.0 3.0 broadcast_select_fusion.3
  337.0 48.2 %collective-permute-done.4 = f32[8,8,16,1024]{3,2,1,0:T(8,128)} collective-permute-done((f32[8,8,16,1024]{3,2,1,0:T(8,128)}, f32[8,8,16,1024]{3,2,1,0:T(8,128)}, u32[]{:S(2)}, u32[]{:S(2)}) %collective-permute-start.4) | collective-permute-done | bytes 4194336 | tf_op jit(solution)/shard_map/ppermute | solution.py:27
  385.2 7.8 %pad_maximum_fusion = f32[8,8,16,2048]{3,2,1,0:T(8,128)} fusion(f32[8,8,16,1024]{3,2,1,0:T(8,128)} %broadcast_select_fusion.3, f32[8,8,16,1024]{3,2,1,0:T(8,128)} %collective-permute-done.4), kind=kLoop, calls=%fused_computation.3 | loop fusion | flops 2097152 | bytes 16777216 | tf_op jit(solution)/shard_map/concatenate | solution.py:62
  393.1 35.2 %while.1 = (s32[]{:T(128)}, f32[8,8,16,2048]{3,2,1,0:T(8,128)}, s32[8,4]{0,1:T(4,128)S(1)}, f32[8,8,16,1024]{3,1,2,0:T(8,128)}, s32[]{:T(128)}) while((s32[]{:T(128)}, f32[8,8,16,2048]{3,2,1,0:T(8,128)}, s32[8,4]{0,1:T(4,128)S(1)}, f32[8,8,16,1024]{3,1,2,0:T(8,128)}, s32[]{:T(128)}) %tuple.25), condition=%wide.while_cond, body=%wide.while_body.sunk | while | flops 2 | bytes 2097785 | solution.py:65
  393.7 2.6 constant_dynamic-slice_fusion.5
  396.3 1.2 copy_dynamic-update-slice_fusion.2
  398.2 2.6 constant_dynamic-slice_fusion.5
  400.8 1.1 copy_dynamic-update-slice_fusion.2
  402.6 2.6 constant_dynamic-slice_fusion.5
  405.2 1.1 copy_dynamic-update-slice_fusion.2
  407.0 2.6 constant_dynamic-slice_fusion.5
  409.6 1.1 copy_dynamic-update-slice_fusion.2
  411.4 2.6 constant_dynamic-slice_fusion.5
  414.0 1.1 copy_dynamic-update-slice_fusion.2
  415.7 2.6 constant_dynamic-slice_fusion.5
  418.4 1.1 copy_dynamic-update-slice_fusion.2
  420.1 2.6 constant_dynamic-slice_fusion.5
  422.7 1.1 copy_dynamic-update-slice_fusion.2
  424.5 2.6 constant_dynamic-slice_fusion.5
  428.2 1.4 fusion.37
  430.2 6.2 collective-permute-done.5
  436.4 2.0 collective-permute-done.6
  438.4 7.8 %fusion.10 = f32[8,8,16,1024]{3,1,2,0:T(8,128)S(1)} fusion(f32[8,8,16,1024]{3,1,2,0:T(8,128)} %get-tuple-element.12, f32[8,8,16,1]{3,1,2,0:T(8,128)S(1)} %collective-permute-done.6, f32[8,8,16,1]{3,1,2,0:T(8,128)S(1)} %collective-permute-done.5, f32[8]{0:T(128)S(1)} %get-tuple-element.30, f32[8]{0:T(128)S(1)} %get-tuple-element.29), kind=kLoop, calls=%fused_computation.17 | loop fusion | flops 14680064 | bytes 8396864 | tf_op jit(solution)/shard_map/sub | solution.py:72
  446.4 1.3 collective-permute-start.7
  447.7 4.8 collective-permute-start.8
  452.4 10.1 %collective-permute-done.7 = f32[1,8,16,1024]{3,1,2,0:T(8,128)S(1)} collective-permute-done((f32[1,8,16,1024]{3,1,2,0:T(8,128)S(1)}, f32[1,8,16,1024]{3,1,2,0:T(8,128)S(1)}, u32[]{:S(2)}, u32[]{:S(2)}) %collective-permute-start.7) | collective-permute-done | bytes 524320 | tf_op jit(solution)/shard_map/ppermute | solution.py:17
  462.6 10.1 %collective-permute-done.8 = f32[1,8,16,1024]{3,1,2,0:T(8,128)S(1)} collective-permute-done((f32[1,8,16,1024]{3,1,2,0:T(8,128)S(1)}, f32[1,8,16,1024]{3,1,2,0:T(8,128)S(1)}, u32[]{:S(2)}, u32[]{:S(2)}) %collective-permute-start.8) | collective-permute-done | bytes 524320 | tf_op jit(solution)/shard_map/ppermute | solution.py:15
  472.6 6.0 bitcast_add_fusion
  478.7 26.5 %copy.39 = f32[8,8,16,1024]{2,1,0,3:T(8,128)} copy(f32[8,8,16,1024]{3,1,2,0:T(8,128)} %bitcast_add_fusion) | data formatting | bytes 8388608 | tf_op jit(solution)/shard_map/add | solution.py:35
  505.2 18.2 %reshape.38 = f32[8,1,131072]{2,1,0:T(1,128)} reshape(f32[1024,8,8,16]{3,2,1,0:T(8,128)} %bitcast.39) | data formatting | bytes 8388608
  523.5 55.4 %all_to_all.36 = f32[8,1,131072]{2,1,0:T(1,128)} all-to-all(f32[8,1,131072]{2,1,0:T(1,128)} %reshape.38), channel_id=1, replica_groups=mesh['rad'=8,'azi'=16] {'rad'}, dimensions={0} | all-to-all | bytes 8388608 | tf_op jit(solution)/shard_map/all_to_all | solution.py:76
  579.4 13.7 %reduce = f32[8,131072]{1,0:T(8,128)} reduce(f32[8,1,131072]{2,1,0:T(1,128)} %all_to_all.36, f32[]{:T(128)} %broadcast.99), dimensions={1}, to_apply=%all_to_all.26.reduce_sub_computation | reduce | bytes 8388612 | tf_op jit(solution)/shard_map/all_to_all | solution.py:76
  593.1 24.3 %reshape.39 = f32[1024,8,8,16]{3,2,1,0:T(8,128)} reshape(f32[8,131072]{1,0:T(8,128)} %reduce) | data formatting | bytes 8388608
  617.4 21.1 %copy.40 = f32[8,8,16,8,128]{4,0,3,2,1:T(8,128)} copy(f32[8,8,16,8,128]{2,1,0,4,3:T(8,128)} %bitcast.40) | data formatting | bytes 8388608 | tf_op jit(solution)/shard_map/all_to_all | solution.py:76
  638.6 5.4 fusion.19
  644.0 2.4 copy.41
  646.5 51.1 %all_to_all.37 = f32[64,8,16,128]{3,2,1,0:T(8,128)S(1)} all-to-all(f32[64,8,16,128]{3,2,1,0:T(8,128)S(1)} %copy.41), channel_id=1, replica_groups=mesh['rad'=8,'azi'=16] {'rad'}, dimensions={0} | all-to-all | bytes 8388608 | tf_op jit(solution)/shard_map/all_to_all | solution.py:74
  697.6 2.6 copy.50
  (38 shorter events, 8.5 us)
Async XLA Ops:
  0.0 638.6 %copy-start = (f32[8,64,64]{2,1,0:T(8,128)S(1)}, f32[8,64,64]{2,1,0:T(8,128)}, u32[]{:S(2)}) copy-start(f32[8,64,64]{2,1,0:T(8,128)} %param.9) | copy-start | bytes 393220
  0.0 48.1 %collective-permute-start = (f32[8,8,16,1024]{3,2,1,0:T(8,128)}, f32[8,8,16,1024]{3,2,1,0:T(8,128)S(1)}, u32[]{:S(2)}, u32[]{:S(2)}) collective-permute-start(f32[8,8,16,1024]{3,2,1,0:T(8,128)} %param.5), channel_id=1, source_target_pairs={{0,1},{1,2},{2,3},{3,4},{4,5},{5,6},{6,7},{7,8},{8,9},{9,10},{10,1... | collective-permute-start | bytes 12582920 | tf_op jit(solution)/shard_map/ppermute | solution.py:27
  51.3 92.0 %collective-permute-start.1 = (f32[8,8,16,1024]{3,2,1,0:T(8,128)S(1)}, f32[8,8,16,1024]{3,2,1,0:T(8,128)S(1)}, u32[]{:S(2)}, u32[]{:S(2)}) collective-permute-start(f32[8,8,16,1024]{3,2,1,0:T(8,128)S(1)} %broadcast_select_fusion), channel_id=1, source_target_pairs={{0,2},{1,3},{2,4},{3,5},{4,6},{5,7},{6,8},{7,9},{8,10},{9,11},{10,... | collective-permute-start | bytes 12582920 | tf_op jit(solution)/shard_map/ppermute | solution.py:27
  144.8 94.5 %collective-permute-start.2 = (f32[8,8,16,1024]{3,2,1,0:T(8,128)S(1)}, f32[8,8,16,1024]{3,2,1,0:T(8,128)S(1)}, u32[]{:S(2)}, u32[]{:S(2)}) collective-permute-start(f32[8,8,16,1024]{3,2,1,0:T(8,128)S(1)} %broadcast_select_fusion.1), channel_id=1, source_target_pairs={{0,4},{1,5},{2,6},{3,7},{4,8},{5,9},{6,10},{7,11},{8,12},{9,13},{1... | collective-permute-start | bytes 12582920 | tf_op jit(solution)/shard_map/ppermute | solution.py:27
  240.7 93.3 %collective-permute-start.3 = (f32[8,8,16,1024]{3,2,1,0:T(8,128)S(1)}, f32[8,8,16,1024]{3,2,1,0:T(8,128)S(1)}, u32[]{:S(2)}, u32[]{:S(2)}) collective-permute-start(f32[8,8,16,1024]{3,2,1,0:T(8,128)S(1)} %broadcast_select_fusion.2), channel_id=1, source_target_pairs={{0,8},{1,9},{2,10},{3,11},{4,12},{5,13},{6,14},{7,15},{8,0},{9,1},... | collective-permute-start | bytes 12582920 | tf_op jit(solution)/shard_map/ppermute | solution.py:27
  334.0 3.0 copy-start.2
  337.0 48.2 %collective-permute-start.4 = (f32[8,8,16,1024]{3,2,1,0:T(8,128)}, f32[8,8,16,1024]{3,2,1,0:T(8,128)}, u32[]{:S(2)}, u32[]{:S(2)}) collective-permute-start(f32[8,8,16,1024]{3,2,1,0:T(8,128)} %broadcast_select_fusion.3), channel_id=1, source_target_pairs={{0,1},{1,2},{2,3},{3,4},{4,5},{5,6},{6,7},{7,8},{8,9},{9,10},{10,1... | collective-permute-start | bytes 12582920 | tf_op jit(solution)/shard_map/ppermute | solution.py:27
  393.1 37.2 %copy-start.3 = (f32[8]{0:T(128)S(1)}, f32[8]{0:T(128)}, u32[]{:S(2)}) copy-start(f32[8]{0:T(128)} %param.7) | copy-start | bytes 100
  429.7 6.8 collective-permute-start.5
  429.7 8.7 %collective-permute-start.6 = (f32[8,8,16,1]{3,1,2,0:T(8,128)S(1)}, f32[8,8,16,1]{3,1,2,0:T(8,128)S(1)}, u32[]{:S(2)}, u32[]{:S(2)}) collective-permute-start(f32[8,8,16,1]{3,1,2,0:T(8,128)S(1)} %get-tuple-element.28), channel_id=1, source_target_pairs={{0,1},{1,2},{2,3},{3,4},{4,5},{5,6},{6,7},{7,8},{8,9},{9,10},{10,1... | collective-permute-start | bytes 12296 | tf_op jit(solution)/shard_map/ppermute | solution.py:15
  438.4 34.2 %copy-start.1 = (f32[8,8]{1,0:T(8,128)S(1)}, f32[8,8]{1,0:T(8,128)}, u32[]{:S(2)}) copy-start(f32[8,8]{1,0:T(8,128)} %param.8) | copy-start | bytes 772
  446.4 16.2 %collective-permute-start.7 = (f32[1,8,16,1024]{3,1,2,0:T(8,128)S(1)}, f32[1,8,16,1024]{3,1,2,0:T(8,128)S(1)}, u32[]{:S(2)}, u32[]{:S(2)}) collective-permute-start(f32[1,8,16,1024]{3,1,2,0:T(8,128)S(1)} %get-tuple-element.25), channel_id=1, source_target_pairs={{16,0},{32,16},{48,32},{64,48},{80,64},{96,80},{112,96},{17,1},{33... | collective-permute-start | bytes 1572872 | tf_op jit(solution)/shard_map/ppermute | solution.py:17
  447.7 25.0 %collective-permute-start.8 = (f32[1,8,16,1024]{3,1,2,0:T(8,128)S(1)}, f32[1,8,16,1024]{3,1,2,0:T(8,128)S(1)}, u32[]{:S(2)}, u32[]{:S(2)}) collective-permute-start(f32[1,8,16,1024]{3,1,2,0:T(8,128)S(1)} %get-tuple-element.26), channel_id=1, source_target_pairs={{0,16},{16,32},{32,48},{48,64},{64,80},{80,96},{96,112},{1,17},{17... | collective-permute-start | bytes 1572872 | tf_op jit(solution)/shard_map/ppermute | solution.py:15
where the time goes:
time: 703 us; the launch traced here: 700 us
  waiting for transfers between devices  394 us (56%)
  local copies, waits for them, and re-layouts  132 us (19%)
  blocking collectives  106 us (15%)
  other arithmetic  39.2 us (6%)
  starting transfers between devices  16.4 us (2%)
  matrix products  11.5 us (2%)
    ppermute x5, waiting for transfers between devices, from_behind(): return lax.ppermute(value, axis, pairs)  366 us
    all_to_all x1, blocking collectives, per_device(): lax.all_to_all(explicit, 'rad', split_axis=3, concat_axis=0, tiled=True)  55.4 us
    all_to_all x1, blocking collectives, per_device(): lax.all_to_all(implicit_step(radial_solve, lax.all_to_all(explicit, 'rad'...  51.1 us
    unnamed x11, local copies, waits for them, and re-layouts  42.6 us
    gather x32, local copies, waits for them, and re-layouts  35.2 us
    add x1, local copies, waits for them, and re-layouts, radial_term(): advected + jnp.einsum('fg,rgzj->rfzj', coupling, padded[2:] - padded[:-2]...  26.5 us
    all_to_all x2, local copies, waits for them, and re-layouts, per_device(): lax.all_to_all(explicit, 'rad', split_axis=3, concat_axis=0, tiled=True)  21.7 us
    ppermute x2, waiting for transfers between devices, with_halo(): lax.ppermute(head, axis, [((i + 1) % count, i) for i in range(ends)])  16.3 us
  transfers between devices with their start and end apart: 9, of which 9 were waited for; matrix products, arithmetic and copies ran while one was open for 0% of the time, Pallas kernels for 0%

commit v1 on v0

v1 whole, which is shorter than its diff:
```python
import jax
import jax.numpy as jnp
from jax import lax
from jax.experimental import pallas as pl
from jax.experimental.pallas import tpu as pltpu
from jax.sharding import PartitionSpec as P


def face_flux(left, right, speed):
    return 0.5 * speed * (left + right) - 0.5 * jnp.abs(speed) * (right - left)


def remap_advect_kernel(shift_ref, speed_ref, x_ref, o_ref):
    g = pl.program_id(0)
    rows, blocks, cells = x_ref.shape
    lane = lax.broadcasted_iota(jnp.int32, (blocks, cells), 1)
    for i in range(rows):
        r = g * rows + i
        s = shift_ref[r]
        w = speed_ref[r]
        turns = s // cells
        rest = s % cells
        x = x_ref[i]
        y = pltpu.roll(x, rest, 1)
        z = jnp.where(lane >= rest, y, pltpu.roll(y, 1, 0))
        u = pltpu.roll(z, turns, 0)
        l1 = pltpu.roll(u, 1, 1)
        lower = jnp.where(lane == 0, pltpu.roll(l1, 1, 0), l1)
        u1 = pltpu.roll(u, cells - 1, 1)
        upper = jnp.where(lane == cells - 1, pltpu.roll(u1, blocks - 1, 0), u1)
        o_ref[i] = u - (face_flux(u, upper, w) - face_flux(lower, u, w))


def remap_advect(shift, speed, rows_all):
    nr, blocks, cells = rows_all.shape
    rb = 8
    spec = pl.BlockSpec((rb, blocks, cells), lambda g, s, w: (g, 0, 0))
    return pl.pallas_call(
        remap_advect_kernel,
        out_shape=jax.ShapeDtypeStruct(rows_all.shape, rows_all.dtype),
        grid_spec=pltpu.PrefetchScalarGridSpec(
            num_scalar_prefetch=2, grid=(nr // rb,), in_specs=[spec], out_specs=spec
        ),
    )(shift, speed, rows_all)


def per_device(fluid_state, orbit_shift, residual_speed, coupling, radial_solve):
    rows, fields, planes, cells = fluid_state.shape
    nrad = lax.axis_size("rad")
    nazi = lax.axis_size("azi")
    nr = rows * nrad
    nphi = cells * nazi
    zlo = nazi // fields
    zhi = planes // zlo
    x = fluid_state.reshape(rows, fields, zhi, zlo, cells).transpose(2, 1, 3, 0, 4)
    x = x.reshape(zhi * fields * zlo, rows, cells)
    x = lax.all_to_all(x, ("rad", "azi"), split_axis=0, concat_axis=0, tiled=True)
    x = x.reshape(nrad, nazi, rows, cells).transpose(0, 2, 1, 3).reshape(nr, nazi, cells)
    shift = jnp.mod(lax.all_gather(orbit_shift, "rad", tiled=True), nphi).astype(jnp.int32)
    speed = lax.all_gather(residual_speed, "rad", tiled=True)
    adv = remap_advect(shift, speed, x)
    adv = lax.all_to_all(adv, "azi", split_axis=1, concat_axis=1, tiled=True)
    adv = adv.reshape(nr, fields, zlo, cells)
    padded = jnp.pad(adv, ((1, 1), (0, 0), (0, 0), (0, 0)))
    explicit = adv + jnp.einsum(
        "fg,rgzj->rfzj", coupling, padded[2:] - padded[:-2], precision=lax.Precision.HIGHEST
    )
    advanced = jnp.einsum("frk,kfzj->rfzj", radial_solve, explicit, precision=lax.Precision.HIGHEST)
    return lax.all_to_all(advanced, "rad", split_axis=0, concat_axis=2, tiled=True)


def solution(mesh):
    return jax.shard_map(
        per_device,
        mesh=mesh,
        in_specs=(P("rad", None, None, "azi"), P("rad"), P("rad"), P(), P()),
        out_specs=P("rad", None, None, "azi"),
        check_vma=False,
    )
```

time: 703 us -> 256 us (0.36)
  waiting for transfers between devices: 394 us -> 0.01 us
  local copies, waits for them, and re-layouts: 132 us -> 35 us
  blocking collectives: 106 us -> 177 us
  other arithmetic: 39.2 us -> 1.58 us
  Pallas kernels: 0 us -> 11.4 us
    ppermute x9 -> x0, waiting for transfers between devices: 394 us -> none  [the longest x5 366 us: from_behind(): return lax.ppermute(value, axis, pairs)]
    unnamed x0 -> x2, blocking collectives: none -> 70.4 us
    unnamed x11 -> x16, local copies, waits for them, and re-layouts: 42.6 us -> 5.76 us
    gather x32 -> x0, local copies, waits for them, and re-layouts: 35.2 us -> none
    add x1 -> x0, local copies, waits for them, and re-layouts: 26.5 us -> none  [radial_term(): advected + jnp.einsum('fg,rgzj->rfzj', coupling, padded[2:] - padded[:-2]...]
    ppermute x9 -> x0, starting transfers between devices: 16.4 us -> none  [the longest x5 9.8 us: from_behind(): return lax.ppermute(value, axis, pairs)]
    all_to_all x3 -> x2, local copies, waits for them, and re-layouts: 24.3 us -> 10.2 us  [per_device(): lax.all_to_all(advanced, 'rad', split_axis=0, concat_axis=2, tiled=True)]
    all_to_all x1 -> x0, other arithmetic: 13.7 us -> none  [per_device(): lax.all_to_all(explicit, 'rad', split_axis=3, concat_axis=0, tiled=True)]
  transfers between devices with their start and end apart: 9 -> 1, of which waited for: 9 -> 0; matrix products, arithmetic and copies ran while one was open for 0% -> 1% of each run, Pallas kernels for 0% -> 0%
where the time goes in v1:
time: 256 us; the launch traced here: 254 us
  blocking collectives  177 us (69%)
  local copies, waits for them, and re-layouts  35 us (14%)
  matrix products  16.9 us (7%)
  Pallas kernels  11.4 us (4%)
  starting transfers between devices  10.8 us (4%)
    unnamed x2, blocking collectives  70.4 us
    all_to_all x1, blocking collectives, per_device(): adv = lax.all_to_all(adv, 'azi', split_axis=1, concat_axis=1, tiled=True)  53.4 us
    all_to_all x1, blocking collectives, per_device(): lax.all_to_all(advanced, 'rad', split_axis=0, concat_axis=2, tiled=True)  53.3 us
    pallas_call x1, Pallas kernels, remap_advect(): pl.pallas_call(remap_advect_kernel, out_shape=jax.ShapeDtypeStruct(rows_a...  11.4 us
    all_to_all x1, starting transfers between devices, per_device(): lax.all_to_all(x, ('rad', 'azi'), split_axis=0, concat_axis=0, tiled=True)  10.8 us
    all_to_all x2, local copies, waits for them, and re-layouts, per_device(): lax.all_to_all(advanced, 'rad', split_axis=0, concat_axis=2, tiled=True)  10.2 us
    dot_general x1, matrix products, per_device(): jnp.einsum('fg,rgzj->rfzj', coupling, padded[2:] - padded[:-2], precision...  9.93 us
    dot_general x1, matrix products, per_device(): jnp.einsum('frk,kfzj->rfzj', radial_solve, explicit, precision=lax.Precis...  6.95 us
  transfers between devices with their start and end apart: 1, of which 0 were waited for; matrix products, arithmetic and copies ran while one was open for 1% of the time, Pallas kernels for 0%

profile of v1, /device:TPU:16, one launch (start us, length us, event | category | flops | bytes accessed | tf_op | source)
XLA Modules:
  0.0 253.6 jit_solution(15879030194676946411)
XLA Ops:
  0.0 0.0 copy-start
  0.0 4.6 %copy.25 = f32[8,8,16,1024]{3,1,2,0:T(8,128)S(1)} copy(f32[8,8,16,1024]{3,2,1,0:T(8,128)} %param.5) | data formatting | bytes 8388608 | tf_op args[0]
  4.6 4.4 %copy.26 = f32[8,8,2,8,1024]{4,3,2,1,0:T(8,128)} copy(f32[8,8,2,8,1024]{4,1,2,0,3:T(8,128)S(1)} %bitcast.32) | data formatting | bytes 8388608 | tf_op jit(solution)/shard_map/transpose | solution.py:55
  9.0 0.0 copy-start.4
  9.0 0.0 copy-start.2
  9.0 0.0 copy-start.3
  9.0 10.8 %all-to-all-start = ((f32[128,8,1024]{2,1,0:T(8,128)}), f32[128,8,1024]{2,1,0:T(8,128)}, u32[]{:S(2)}, u32[]{:S(2)}) async-start(f32[128,8,1024]{2,1,0:T(8,128)} %bitcast.29), calls=%async_computation | async-start | bytes 8388608 | tf_op jit(solution)/shard_map/all_to_all | solution.py:57
  19.8 0.0 copy-done.4
  19.8 0.7 dynamic-slice
  21.2 0.0 copy-done.2
  21.2 0.2 dynamic-update-slice
  21.4 0.0 copy-done.3
  21.4 0.2 dynamic-update-slice.1
  21.7 51.1 %all-reduce.1 = s32[64]{0:T(128)S(1)} all-reduce(s32[64]{0:T(128)S(1)} %dynamic-update-slice), channel_id=1, replica_groups=mesh['rad'=8,'azi'=16] {'rad'}, use_global_device_ids=true, to_apply=%add.1 | all-reduce | flops 64 | bytes 512
  72.8 19.2 %all-reduce.2.speed_ref = f32[64]{0:T(128)} all-reduce(f32[64]{0:T(128)S(1)} %dynamic-update-slice.1), channel_id=1, replica_groups=mesh['rad'=8,'azi'=16] {'rad'}, use_global_device_ids=true, to_apply=%add.2 | all-reduce | flops 64 | bytes 512
  92.1 0.6 and_select_fusion.shift_ref
  92.7 0.0 all-to-all-done
  92.7 6.7 %copy.27 = f32[8,8,16,1024]{3,2,1,0:T(8,128)} copy(f32[8,8,16,1024]{3,1,2,0:T(8,128)} %bitcast.5) | data formatting | bytes 8388608 | tf_op jit(solution)/shard_map/transpose | solution.py:58
  99.4 11.4 %shard_map.55 = f32[64,16,1024]{2,1,0:T(8,128)} custom-call(s32[64]{0:T(128)} %and_select_fusion.shift_ref, f32[64]{0:T(128)} %all-reduce.2.speed_ref, f32[64,16,1024]{2,1,0:T(8,128)} %bitcast.30), custom_call_target="tpu_custom_call" | custom-call | tf_op jit(solution)/shard_map/pallas_call | solution.py:38
  110.8 4.6 %copy.28 = f32[64,16,1024]{2,0,1:T(8,128)S(1)} copy(f32[64,16,1024]{2,1,0:T(8,128)} %shard_map.55) | data formatting | bytes 8388608 | tf_op jit(solution)/shard_map/pallas_call | solution.py:38
  115.4 53.4 %all_to_all.28 = f32[64,16,1024]{2,0,1:T(8,128)S(1)} all-to-all(f32[64,16,1024]{2,0,1:T(8,128)S(1)} %copy.28), channel_id=1, replica_groups=mesh['rad'=8,'azi'=16] {'azi'}, dimensions={1} | all-to-all | bytes 8388608 | tf_op jit(solution)/shard_map/all_to_all | solution.py:62
  168.9 0.0 copy-start.1
  168.9 1.0 fusion
  169.9 0.0 copy-done.1
  169.9 9.9 %bitcast_add_fusion = f32[64,8,2,1024]{3,1,2,0:T(8,128)S(1)} fusion(f32[64,8,2,1024]{3,0,2,1:T(8,128)S(1)} %bitcast.28, f32[64,8,2,1024]{3,0,2,1:T(8,128)S(1)} %fusion, f32[8,8]{1,0:T(8,128)S(1)} %copy-done.1), kind=kOutput, calls=%fused_computation.3 | convolution fusion | flops 101711872 | bytes 12583168 | tf_op jit(solution)/shard_map/fg,rgzj->rfzj/dot_general | solution.py:65
  179.8 0.0 copy-done
  179.8 7.0 %fusion.7 = f32[64,8,2,1024]{3,0,2,1:T(8,128)S(1)} fusion(f32[64,8,2,1024]{3,1,2,0:T(8,128)S(1)} %bitcast_add_fusion, f32[8,64,64]{2,1,0:T(8,128)S(1)} %copy-done), kind=kOutput, calls=%fused_computation.8 | convolution fusion | flops 805306368 | bytes 8519680 | tf_op jit(solution)/shard_map/frk,kfzj->rfzj/dot_general | solution.py:68
  186.8 3.2 %copy.32 = f32[64,8,2,1024]{3,2,1,0:T(2,128)S(1)} copy(f32[64,8,2,1024]{3,0,2,1:T(8,128)S(1)} %fusion.7) | data formatting | bytes 8388608 | tf_op jit(solution)/shard_map/frk,kfzj->rfzj/transpose | solution.py:68
  190.0 53.3 %all_to_all.29 = f32[64,8,2,1024]{3,2,1,0:T(2,128)S(1)} all-to-all(f32[64,8,2,1024]{3,2,1,0:T(2,128)S(1)} %copy.32), channel_id=1, replica_groups=mesh['rad'=8,'azi'=16] {'rad'}, dimensions={0} | all-to-all | bytes 8388608 | tf_op jit(solution)/shard_map/all_to_all | solution.py:69
  243.3 4.2 %copy.33 = f32[8,8,8,2,1024]{4,3,2,1,0:T(2,128)} copy(f32[8,8,8,2,1024]{4,3,1,0,2:T(2,128)S(1)} %bitcast.31) | data formatting | bytes 8388608 | tf_op jit(solution)/shard_map/all_to_all | solution.py:69
  247.5 6.0 %all_to_all.24 = f32[8,8,16,1024]{3,2,1,0:T(8,128)} reshape(f32[8,8,8,2,1024]{4,3,2,1,0:T(2,128)} %copy.33) | data formatting | bytes 8388608 | tf_op jit(solution)/shard_map/all_to_all | solution.py:69
  (2 shorter events, 0.0 us)
Async XLA Ops:
  0.0 179.8 %copy-start = (f32[8,64,64]{2,1,0:T(8,128)S(1)}, f32[8,64,64]{2,1,0:T(8,128)}, u32[]{:S(2)}) copy-start(f32[8,64,64]{2,1,0:T(8,128)} %param.9) | copy-start | bytes 393220
  9.0 10.8 %copy-start.4 = (u32[128]{0:T(128)S(1)}, u32[128]{0:T(128)}, u32[]{:S(2)}) copy-start(u32[128]{0:T(128)} %constant.22) | copy-start | bytes 1540
  9.0 12.2 %copy-start.2 = (s32[8]{0:T(128)S(1)}, s32[8]{0:T(128)}, u32[]{:S(2)}) copy-start(s32[8]{0:T(128)} %param.6) | copy-start | bytes 100
  9.0 12.4 %copy-start.3 = (f32[8]{0:T(128)S(1)}, f32[8]{0:T(128)}, u32[]{:S(2)}) copy-start(f32[8]{0:T(128)} %param.7) | copy-start | bytes 100
  9.0 83.7 %all-to-all-start = ((f32[128,8,1024]{2,1,0:T(8,128)}), f32[128,8,1024]{2,1,0:T(8,128)}, u32[]{:S(2)}, u32[]{:S(2)}) async-start(f32[128,8,1024]{2,1,0:T(8,128)} %bitcast.29), calls=%async_computation | async-start | bytes 8388608 | tf_op jit(solution)/shard_map/all_to_all | solution.py:57
  168.9 1.0 copy-start.1

commit v2 on v1

--- a/solution.py
+++ b/solution.py
@@ -14,7 +14,8 @@
     g = pl.program_id(0)
     rows, blocks, cells = x_ref.shape
     lane = lax.broadcasted_iota(jnp.int32, (blocks, cells), 1)
-    for i in range(rows):
+
+    def body(i, carry):
         r = g * rows + i
         s = shift_ref[r]
         w = speed_ref[r]
@@ -29,6 +30,9 @@
         u1 = pltpu.roll(u, cells - 1, 1)
         upper = jnp.where(lane == cells - 1, pltpu.roll(u1, blocks - 1, 0), u1)
         o_ref[i] = u - (face_flux(u, upper, w) - face_flux(lower, u, w))
+        return carry
+
+    lax.fori_loop(0, rows, body, 0)
 
 
 def remap_advect(shift, speed, rows_all):
@@ -41,6 +45,9 @@
         grid_spec=pltpu.PrefetchScalarGridSpec(
             num_scalar_prefetch=2, grid=(nr // rb,), in_specs=[spec], out_specs=spec
         ),
+        cost_estimate=pl.CostEstimate(
+            flops=30 * rows_all.size, bytes_accessed=8 * rows_all.size, transcendentals=0
+        ),
     )(shift, speed, rows_all)
 
 
@@ -50,23 +57,36 @@
     nazi = lax.axis_size("azi")
     nr = rows * nrad
     nphi = cells * nazi
-    zlo = nazi // fields
-    zhi = planes // zlo
-    x = fluid_state.reshape(rows, fields, zhi, zlo, cells).transpose(2, 1, 3, 0, 4)
-    x = x.reshape(zhi * fields * zlo, rows, cells)
-    x = lax.all_to_all(x, ("rad", "azi"), split_axis=0, concat_axis=0, tiled=True)
-    x = x.reshape(nrad, nazi, rows, cells).transpose(0, 2, 1, 3).reshape(nr, nazi, cells)
-    shift = jnp.mod(lax.all_gather(orbit_shift, "rad", tiled=True), nphi).astype(jnp.int32)
-    speed = lax.all_gather(residual_speed, "rad", tiled=True)
-    adv = remap_advect(shift, speed, x)
-    adv = lax.all_to_all(adv, "azi", split_axis=1, concat_axis=1, tiled=True)
-    adv = adv.reshape(nr, fields, zlo, cells)
-    padded = jnp.pad(adv, ((1, 1), (0, 0), (0, 0), (0, 0)))
-    explicit = adv + jnp.einsum(
-        "fg,rgzj->rfzj", coupling, padded[2:] - padded[:-2], precision=lax.Precision.HIGHEST
-    )
-    advanced = jnp.einsum("frk,kfzj->rfzj", radial_solve, explicit, precision=lax.Precision.HIGHEST)
-    return lax.all_to_all(advanced, "rad", split_axis=0, concat_axis=2, tiled=True)
+    halves = nazi // fields
+    part = rows // halves
+    pc = nrad
+    chunks = planes // pc
+    table = jnp.stack([orbit_shift.astype(jnp.float32), residual_speed])
+    table = lax.all_gather(table, "rad", axis=1, tiled=True)
+    shift_all = jnp.mod(table[0].astype(jnp.int32), nphi)
+    speed_all = table[1]
+    h = lax.axis_index("azi") % halves
+    order = (jnp.arange(nrad)[:, None] * rows + h * part + jnp.arange(part)[None, :]).reshape(-1)
+    shift = shift_all[order]
+    speed = speed_all[order]
+    outs = []
+    for c in range(chunks):
+        xc = fluid_state[:, :, c * pc:(c + 1) * pc, :]
+        xc = xc.reshape(halves, part, fields, pc, cells).transpose(3, 2, 0, 1, 4)
+        xc = xc.reshape(pc * fields * halves, part, cells)
+        xc = lax.all_to_all(xc, ("rad", "azi"), split_axis=0, concat_axis=0, tiled=True)
+        xc = xc.reshape(nrad, nazi, part, cells).transpose(0, 2, 1, 3).reshape(nrad * part, nazi, cells)
+        adv = remap_advect(shift, speed, xc)
+        adv = lax.all_to_all(adv, "azi", split_axis=1, concat_axis=1, tiled=True)
+        adv = adv.reshape(nrad, part, fields, halves, cells).transpose(0, 3, 1, 2, 4).reshape(nr, fields, cells)
+        padded = jnp.pad(adv, ((1, 1), (0, 0), (0, 0)))
+        explicit = adv + jnp.einsum(
+            "fg,rgj->rfj", coupling, padded[2:] - padded[:-2], precision=lax.Precision.HIGHEST
+        )
+        advanced = jnp.einsum("frk,kfj->rfj", radial_solve, explicit, precision=lax.Precision.HIGHEST)
+        advanced = advanced.reshape(nr, fields, 1, cells)
+        outs.append(lax.all_to_all(advanced, "rad", split_axis=0, concat_axis=2, tiled=True))
+    return jnp.concatenate(outs, axis=2)
 
 
 def solution(mesh):

time: 256 us -> 254 us (level)
  blocking collectives: 177 us -> 35 us
  waiting for transfers between devices: 0.01 us -> 95.4 us
  starting transfers between devices: 10.8 us -> 38.6 us
  local copies, waits for them, and re-layouts: 35 us -> 52 us
  Pallas kernels: 11.4 us -> 18.7 us
  matrix products: 16.9 us -> 11.3 us
    all_to_all x2 -> x0, blocking collectives: 107 us -> none  [the longest x1 53.4 us: per_device(): adv = lax.all_to_all(adv, 'azi', split_axis=1, concat_axis=1, tiled=True)]
    all_to_all x1 -> x6, waiting for transfers between devices: 0.01 us -> 95.4 us  [the longest x2 47.2 us: per_device(): lax.all_to_all(advanced, 'rad', split_axis=0, concat_axis=2, tiled=True)]
    unnamed x2 -> x0, blocking collectives: 70.4 us -> none
    all_gather x0 -> x1, blocking collectives: none -> 35 us  [per_device(): table = lax.all_gather(table, 'rad', axis=1, tiled=True)]
    all_to_all x1 -> x6, starting transfers between devices: 10.8 us -> 38.6 us  [the longest x2 16.5 us: per_device(): lax.all_to_all(xc, ('rad', 'azi'), split_axis=0, concat_axis=0, tiled=True)]
    reshape x0 -> x8, local copies, waits for them, and re-layouts: none -> 23 us  [the longest x4 11 us: per_device(): adv.reshape(nrad, part, fields, halves, cells).transpose(0, 3, 1, 2, 4)]
    transpose x3 -> x2, local copies, waits for them, and re-layouts: 14.4 us -> 2.96 us  [per_device(): xc.reshape(nrad, nazi, part, cells).transpose(0, 2, 1, 3)]
    pallas_call x1 -> x2, Pallas kernels: 11.4 us -> 18.7 us  [remap_advect(): pl.pallas_call(remap_advect_kernel, out_shape=jax.ShapeDtypeStruct(rows_a...]
  transfers between devices with their start and end apart: 1 -> 6, of which waited for: 0 -> 5; matrix products, arithmetic and copies ran while one was open for 1% -> 21% of each run, Pallas kernels for 0% -> 7%
where the time goes in v2:
time: 254 us
  waiting for transfers between devices  95.4 us (38%)
  local copies, waits for them, and re-layouts  52 us (20%)
  starting transfers between devices  38.6 us (15%)
  blocking collectives  35 us (14%)
  Pallas kernels  18.7 us (7%)
  matrix products  11.3 us (4%)
    all_to_all x2, waiting for transfers between devices, per_device(): lax.all_to_all(advanced, 'rad', split_axis=0, concat_axis=2, tiled=True)  47.2 us
    all_gather x1, blocking collectives, per_device(): table = lax.all_gather(table, 'rad', axis=1, tiled=True)  35 us
    all_to_all x2, waiting for transfers between devices, per_device(): lax.all_to_all(xc, ('rad', 'azi'), split_axis=0, concat_axis=0, tiled=True)  24.4 us
    all_to_all x2, waiting for transfers between devices, per_device(): adv = lax.all_to_all(adv, 'azi', split_axis=1, concat_axis=1, tiled=True)  23.8 us
    pallas_call x2, Pallas kernels, remap_advect(): pl.pallas_call(remap_advect_kernel, out_shape=jax.ShapeDtypeStruct(rows_a...  18.7 us
    all_to_all x2, starting transfers between devices, per_device(): lax.all_to_all(xc, ('rad', 'azi'), split_axis=0, concat_axis=0, tiled=True)  16.5 us
    all_to_all x2, starting transfers between devices, per_device(): adv = lax.all_to_all(adv, 'azi', split_axis=1, concat_axis=1, tiled=True)  14 us
    reshape x4, local copies, waits for them, and re-layouts, per_device(): adv.reshape(nrad, part, fields, halves, cells).transpose(0, 3, 1, 2, 4)  11 us
  transfers between devices with their start and end apart: 6, of which 5 were waited for; matrix products, arithmetic and copies ran while one was open for 21% of the time, Pallas kernels for 7%

profile of v2, /device:TPU:16, one launch (start us, length us, event | category | flops | bytes accessed | tf_op | source)
XLA Modules:
  0.0 253.6 jit_solution(11360192308286765295)
XLA Ops:
  0.0 0.0 copy-start
  0.0 4.0 %fusion.30 = (f32[8,8,8,1024]{3,2,1,0:T(8,128)}, f32[8,8,8,1024]{3,2,1,0:T(8,128)S(1)}) fusion(f32[8,8,16,1024]{3,2,1,0:T(8,128)} %param.5), kind=kLoop, calls=%fused_computation.39 | loop fusion | bytes 8388608 | tf_op jit(solution)/shard_map/slice | solution.py:74
  4.0 2.7 %copy.31 = f32[2,4,8,8,1024]{4,1,0,2,3:T(4,128)} copy(f32[2,4,8,8,1024]{4,3,2,1,0:T(8,128)S(1)} %bitcast.84) | data formatting | bytes 4194304 | tf_op jit(solution)/shard_map/reshape | solution.py:75
  6.7 10.3 %all-to-all-start.3 = ((f32[128,4,1024]{2,1,0:T(4,128)}), f32[128,4,1024]{2,1,0:T(4,128)S(1)}, u32[]{:S(2)}, u32[]{:S(2)}) async-start(f32[128,4,1024]{2,1,0:T(4,128)} %bitcast.79), calls=%async_computation.3 | async-start | bytes 4194304 | tf_op jit(solution)/shard_map/all_to_all | solution.py:77
  17.1 4.3 %copy.23 = f32[2,4,8,8,1024]{4,1,0,2,3:T(4,128)} copy(f32[2,4,8,8,1024]{4,3,2,1,0:T(8,128)} %bitcast.82) | data formatting | bytes 4194304 | tf_op jit(solution)/shard_map/reshape | solution.py:75
  21.3 24.4 %all-to-all-done.3 = f32[128,4,1024]{2,1,0:T(4,128)S(1)} async-done(((f32[128,4,1024]{2,1,0:T(4,128)}), f32[128,4,1024]{2,1,0:T(4,128)S(1)}, u32[]{:S(2)}, u32[]{:S(2)}) %all-to-all-start.3) | async-done | bytes 2097184 | tf_op jit(solution)/shard_map/all_to_all | solution.py:77
  45.7 1.3 copy-done.1
  47.0 6.2 %all-to-all-start = ((f32[128,4,1024]{2,1,0:T(4,128)}), f32[128,4,1024]{2,1,0:T(4,128)S(1)}, u32[]{:S(2)}, u32[]{:S(2)}) async-start(f32[128,4,1024]{2,1,0:T(4,128)} %bitcast.77), calls=%async_computation | async-start | bytes 4194304 | tf_op jit(solution)/shard_map/all_to_all | solution.py:77
  53.2 0.1 iota_add_fusion
  53.3 0.1 add.73
  53.4 0.0 copy-done.5
  53.4 0.0 copy-done.4
  53.4 35.0 %all-gather = f32[8,8,2]{1,2,0:T(2,128)S(1)} all-gather(f32[1,8,2]{1,2,0:T(2,128)S(1)} %maximum_bitcast_fusion), channel_id=1, replica_groups=mesh['rad'=8,'azi'=16] {'rad'}, dimensions={0}, use_global_device_ids=true | all-gather | bytes 576 | tf_op jit(solution)/shard_map/all_gather | solution.py:65
  88.4 0.1 reshape.111
  88.6 1.2 gather_fusion
  89.8 1.2 gather_fusion.1
  91.0 2.8 %copy.32 = f32[128,4,1024]{2,0,1:T(8,128)S(1)} copy(f32[128,4,1024]{2,1,0:T(4,128)} %copy-done.1) | data formatting | bytes 4194304 | tf_op jit(solution)/shard_map/all_to_all | solution.py:77
  93.8 1.5 copy.33
  95.3 9.4 %shard_map.56 = f32[32,16,1024]{2,1,0:T(8,128)} custom-call(s32[32]{0:T(128)} %gather_fusion, f32[32]{0:T(128)} %gather_fusion.1, f32[32,16,1024]{2,1,0:T(8,128)} %bitcast.76), custom_call_target="tpu_custom_call" | custom-call | flops 15728640 | bytes 4194304 | tf_op jit(solution)/shard_map/pallas_call | solution.py:42
  104.6 4.1 %copy.34 = f32[32,16,1024]{2,0,1:T(8,128)} copy(f32[32,16,1024]{2,1,0:T(8,128)} %shard_map.56) | data formatting | bytes 4194304 | tf_op jit(solution)/shard_map/pallas_call | solution.py:42
  108.8 0.0 all-to-all-done
  108.8 7.3 %all-to-all-start.4 = ((f32[32,16,1024]{2,0,1:T(8,128)}), f32[32,16,1024]{2,0,1:T(8,128)}, u32[]{:S(2)}, u32[]{:S(2)}) async-start(f32[32,16,1024]{2,0,1:T(8,128)} %copy.34), calls=%async_computation.4 | async-start | bytes 4194304 | tf_op jit(solution)/shard_map/all_to_all | solution.py:80
  116.1 1.2 copy.24
  117.3 1.5 copy.25
  118.8 9.4 %shard_map.55 = f32[32,16,1024]{2,1,0:T(8,128)} custom-call(s32[32]{0:T(128)} %gather_fusion, f32[32]{0:T(128)} %gather_fusion.1, f32[32,16,1024]{2,1,0:T(8,128)} %bitcast.75), custom_call_target="tpu_custom_call" | custom-call | flops 15728640 | bytes 4194304 | tf_op jit(solution)/shard_map/pallas_call | solution.py:42
  128.2 4.2 %copy.26 = f32[32,16,1024]{2,0,1:T(8,128)} copy(f32[32,16,1024]{2,1,0:T(8,128)} %shard_map.55) | data formatting | bytes 4194304 | tf_op jit(solution)/shard_map/pallas_call | solution.py:42
  132.3 11.0 %all-to-all-done.4 = f32[32,16,1024]{2,0,1:T(8,128)} async-done(((f32[32,16,1024]{2,0,1:T(8,128)}), f32[32,16,1024]{2,0,1:T(8,128)}, u32[]{:S(2)}, u32[]{:S(2)}) %all-to-all-start.4) | async-done | bytes 2097184 | tf_op jit(solution)/shard_map/all_to_all | solution.py:80
  143.3 6.7 %all-to-all-start.1 = ((f32[32,16,1024]{2,0,1:T(8,128)}), f32[32,16,1024]{2,0,1:T(8,128)S(1)}, u32[]{:S(2)}, u32[]{:S(2)}) async-start(f32[32,16,1024]{2,0,1:T(8,128)} %copy.26), calls=%async_computation.1 | async-start | bytes 4194304 | tf_op jit(solution)/shard_map/all_to_all | solution.py:80
  150.0 2.8 %reshape.91 = f32[8,4,8,2,1024]{4,1,0,3,2:T(4,128)} reshape(f32[32,16,1024]{2,0,1:T(8,128)} %all-to-all-done.4) | data formatting | bytes 4194304 | tf_op jit(solution)/shard_map/reshape | solution.py:81
  152.8 3.2 %copy.35 = f32[8,4,8,2,1024]{4,2,1,3,0:T(8,128)S(1)} copy(f32[8,4,8,2,1024]{4,1,0,3,2:T(4,128)} %reshape.91) | data formatting | bytes 4194304 | tf_op jit(solution)/shard_map/reshape | solution.py:81
  156.0 0.0 copy-done.3
  156.1 2.4 bitcast_add_fusion
  158.4 3.3 %fusion.21 = f32[64,8,1,1024]{3,0,1,2:T(8,128)S(1)} fusion(f32[8,64,64]{2,1,0:T(8,128)S(1)} %copy-done, f32[64,8,1024]{2,1,0:T(8,128)S(1)} %bitcast_add_fusion), kind=kOutput, calls=%fused_computation.22 | convolution fusion | flops 402653184 | bytes 4325376 | tf_op jit(solution)/shard_map/frk,kfj->rfj/dot_general | solution.py:86
  161.7 2.5 copy.37
  164.3 12.8 %all-to-all-done.1 = f32[32,16,1024]{2,0,1:T(8,128)S(1)} async-done(((f32[32,16,1024]{2,0,1:T(8,128)}), f32[32,16,1024]{2,0,1:T(8,128)S(1)}, u32[]{:S(2)}, u32[]{:S(2)}) %all-to-all-start.1) | async-done | bytes 2097184 | tf_op jit(solution)/shard_map/all_to_all | solution.py:80
  177.1 4.6 %all-to-all-start.5 = ((f32[64,8,1,1024]{3,1,2,0:T(8,128)}), f32[64,8,1,1024]{3,1,2,0:T(8,128)}, u32[]{:S(2)}, u32[]{:S(2)}) async-start(f32[64,8,1,1024]{3,1,2,0:T(8,128)} %copy.37), calls=%async_computation.5 | async-start | bytes 4194304 | tf_op jit(solution)/shard_map/all_to_all | solution.py:88
  181.7 1.6 reshape.84
  183.3 3.2 %copy.27 = f32[8,4,8,2,1024]{4,2,1,3,0:T(8,128)S(1)} copy(f32[8,4,8,2,1024]{4,1,0,3,2:T(4,128)} %reshape.84) | data formatting | bytes 4194304 | tf_op jit(solution)/shard_map/reshape | solution.py:81
  186.5 2.4 bitcast_add_fusion.1
  188.9 3.3 %fusion.18 = f32[64,8,1,1024]{3,0,1,2:T(8,128)S(1)} fusion(f32[8,64,64]{2,1,0:T(8,128)S(1)} %copy-done, f32[64,8,1024]{2,1,0:T(8,128)S(1)} %bitcast_add_fusion.1), kind=kOutput, calls=%fused_computation.21 | convolution fusion | flops 402653184 | bytes 4325376 | tf_op jit(solution)/shard_map/frk,kfj->rfj/dot_general | solution.py:86
  192.2 2.5 %copy.29 = f32[64,8,1,1024]{3,1,2,0:T(8,128)} copy(f32[64,8,1,1024]{3,0,1,2:T(8,128)S(1)} %fusion.18) | data formatting | bytes 4194304 | tf_op jit(solution)/shard_map/reshape | solution.py:87
  194.7 19.5 %all-to-all-done.5 = f32[64,8,1,1024]{3,1,2,0:T(8,128)} async-done(((f32[64,8,1,1024]{3,1,2,0:T(8,128)}), f32[64,8,1,1024]{3,1,2,0:T(8,128)}, u32[]{:S(2)}, u32[]{:S(2)}) %all-to-all-start.5) | async-done | bytes 2097184 | tf_op jit(solution)/shard_map/all_to_all | solution.py:88
  214.2 3.6 %all-to-all-start.2 = ((f32[64,8,1,1024]{3,1,2,0:T(8,128)}), f32[64,8,1,1024]{3,1,2,0:T(8,128)S(1)}, u32[]{:S(2)}, u32[]{:S(2)}) async-start(f32[64,8,1,1024]{3,1,2,0:T(8,128)} %copy.29), calls=%async_computation.2 | async-start | bytes 4194304 | tf_op jit(solution)/shard_map/all_to_all | solution.py:88
  217.8 4.2 %copy.49 = f32[8,8,8,1,1024]{4,0,2,1,3:T(8,128)} copy(f32[8,8,8,1,1024]{4,2,1,0,3:T(8,128)} %bitcast.36) | data formatting | bytes 4194304 | tf_op jit(solution)/shard_map/all_to_all | solution.py:88
  222.0 27.7 %all-to-all-done.2 = f32[64,8,1,1024]{3,1,2,0:T(8,128)S(1)} async-done(((f32[64,8,1,1024]{3,1,2,0:T(8,128)}), f32[64,8,1,1024]{3,1,2,0:T(8,128)S(1)}, u32[]{:S(2)}, u32[]{:S(2)}) %all-to-all-start.2) | async-done | bytes 2097184 | tf_op jit(solution)/shard_map/all_to_all | solution.py:88
  249.7 1.3 copy.50
  251.0 0.3 copy-done.2
  251.3 2.3 pad_maximum_fusion
  (14 shorter events, 0.1 us)
Async XLA Ops:
  0.0 158.4 %copy-start = (f32[8,64,64]{2,1,0:T(8,128)S(1)}, f32[8,64,64]{2,1,0:T(8,128)}, u32[]{:S(2)}) copy-start(f32[8,64,64]{2,1,0:T(8,128)} %param.9) | copy-start | bytes 393220
  6.7 39.0 %all-to-all-start.3 = ((f32[128,4,1024]{2,1,0:T(4,128)}), f32[128,4,1024]{2,1,0:T(4,128)S(1)}, u32[]{:S(2)}, u32[]{:S(2)}) async-start(f32[128,4,1024]{2,1,0:T(4,128)} %bitcast.79), calls=%async_computation.3 | async-start | bytes 4194304 | tf_op jit(solution)/shard_map/all_to_all | solution.py:77
  45.7 1.3 copy-start.1
  45.7 7.7 %copy-start.5 = (s32[8]{0:T(128)S(1)}, s32[8]{0:T(128)}, u32[]{:S(2)}) copy-start(s32[8]{0:T(128)} %param.6) | copy-start | bytes 100
  45.7 7.7 %copy-start.4 = (f32[8]{0:T(128)S(1)}, f32[8]{0:T(128)}, u32[]{:S(2)}) copy-start(f32[8]{0:T(128)} %param.7) | copy-start | bytes 100
  47.0 61.7 %all-to-all-start = ((f32[128,4,1024]{2,1,0:T(4,128)}), f32[128,4,1024]{2,1,0:T(4,128)S(1)}, u32[]{:S(2)}, u32[]{:S(2)}) async-start(f32[128,4,1024]{2,1,0:T(4,128)} %bitcast.77), calls=%async_computation | async-start | bytes 4194304 | tf_op jit(solution)/shard_map/all_to_all | solution.py:77
  108.8 34.5 %all-to-all-start.4 = ((f32[32,16,1024]{2,0,1:T(8,128)}), f32[32,16,1024]{2,0,1:T(8,128)}, u32[]{:S(2)}, u32[]{:S(2)}) async-start(f32[32,16,1024]{2,0,1:T(8,128)} %copy.34), calls=%async_computation.4 | async-start | bytes 4194304 | tf_op jit(solution)/shard_map/all_to_all | solution.py:80
  143.3 33.8 %all-to-all-start.1 = ((f32[32,16,1024]{2,0,1:T(8,128)}), f32[32,16,1024]{2,0,1:T(8,128)S(1)}, u32[]{:S(2)}, u32[]{:S(2)}) async-start(f32[32,16,1024]{2,0,1:T(8,128)} %copy.26), calls=%async_computation.1 | async-start | bytes 4194304 | tf_op jit(solution)/shard_map/all_to_all | solution.py:80
  152.8 3.2 %copy-start.3 = (f32[8,8]{1,0:T(8,128)S(1)}, f32[8,8]{1,0:T(8,128)}, u32[]{:S(2)}) copy-start(f32[8,8]{1,0:T(8,128)} %param.8) | copy-start | bytes 772
  177.1 37.2 %all-to-all-start.5 = ((f32[64,8,1,1024]{3,1,2,0:T(8,128)}), f32[64,8,1,1024]{3,1,2,0:T(8,128)}, u32[]{:S(2)}, u32[]{:S(2)}) async-start(f32[64,8,1,1024]{3,1,2,0:T(8,128)} %copy.37), calls=%async_computation.5 | async-start | bytes 4194304 | tf_op jit(solution)/shard_map/all_to_all | solution.py:88
  214.2 35.5 %all-to-all-start.2 = ((f32[64,8,1,1024]{3,1,2,0:T(8,128)}), f32[64,8,1,1024]{3,1,2,0:T(8,128)S(1)}, u32[]{:S(2)}, u32[]{:S(2)}) async-start(f32[64,8,1,1024]{3,1,2,0:T(8,128)} %copy.29), calls=%async_computation.2 | async-start | bytes 4194304 | tf_op jit(solution)/shard_map/all_to_all | solution.py:88
  249.7 1.6 copy-start.2

commit v3 on v2

--- a/solution.py
+++ b/solution.py
@@ -69,12 +69,15 @@
     order = (jnp.arange(nrad)[:, None] * rows + h * part + jnp.arange(part)[None, :]).reshape(-1)
     shift = shift_all[order]
     speed = speed_all[order]
-    outs = []
+    sends = []
     for c in range(chunks):
         xc = fluid_state[:, :, c * pc:(c + 1) * pc, :]
         xc = xc.reshape(halves, part, fields, pc, cells).transpose(3, 2, 0, 1, 4)
-        xc = xc.reshape(pc * fields * halves, part, cells)
-        xc = lax.all_to_all(xc, ("rad", "azi"), split_axis=0, concat_axis=0, tiled=True)
+        sends.append(xc.reshape(pc * fields * halves, part, cells))
+    shift, speed, sends[0] = lax.optimization_barrier((shift, speed, sends[0]))
+    outs = []
+    for c in range(chunks):
+        xc = lax.all_to_all(sends[c], ("rad", "azi"), split_axis=0, concat_axis=0, tiled=True)
         xc = xc.reshape(nrad, nazi, part, cells).transpose(0, 2, 1, 3).reshape(nrad * part, nazi, cells)
         adv = remap_advect(shift, speed, xc)
         adv = lax.all_to_all(adv, "azi", split_axis=1, concat_axis=1, tiled=True)

time: 254 us -> 250 us (0.984)
  blocking collectives: 35 us -> 19.2 us
  waiting for transfers between devices: 95.4 us -> 107 us
  starting transfers between devices: 38.6 us -> 34.5 us
    all_gather x1, blocking collectives: 35 us -> 19.2 us  [per_device(): table = lax.all_gather(table, 'rad', axis=1, tiled=True)]
    all_to_all x2, waiting for transfers between devices: 24.4 us -> 35.3 us  [per_device(): lax.all_to_all(sends[c], ('rad', 'azi'), split_axis=0, concat_axis=0, til...]
    all_to_all x2, starting transfers between devices: 16.5 us -> 13.6 us  [per_device(): lax.all_to_all(sends[c], ('rad', 'azi'), split_axis=0, concat_axis=0, til...]
  transfers between devices with their start and end apart: 6 -> 6, of which waited for: 5 -> 6; matrix products, arithmetic and copies ran while one was open for 21% -> 20% of each run, Pallas kernels for 7% -> 8%
where the time goes in v3:
time: 250 us; the launch traced here: 249 us
  waiting for transfers between devices  107 us (43%)
  local copies, waits for them, and re-layouts  54.5 us (22%)
  starting transfers between devices  34.5 us (14%)
  blocking collectives  19.2 us (8%)
  Pallas kernels  18.7 us (7%)
  matrix products  11.3 us (5%)
  other arithmetic  3.79 us (2%)
    all_to_all x2, waiting for transfers between devices, per_device(): lax.all_to_all(advanced, 'rad', split_axis=0, concat_axis=2, tiled=True)  47.7 us
    all_to_all x2, waiting for transfers between devices, per_device(): lax.all_to_all(sends[c], ('rad', 'azi'), split_axis=0, concat_axis=0, til...  35.3 us
    all_to_all x2, waiting for transfers between devices, per_device(): adv = lax.all_to_all(adv, 'azi', split_axis=1, concat_axis=1, tiled=True)  23.5 us
    all_gather x1, blocking collectives, per_device(): table = lax.all_gather(table, 'rad', axis=1, tiled=True)  19.2 us
    pallas_call x2, Pallas kernels, remap_advect(): pl.pallas_call(remap_advect_kernel, out_shape=jax.ShapeDtypeStruct(rows_a...  18.7 us
    all_to_all x2, starting transfers between devices, per_device(): lax.all_to_all(sends[c], ('rad', 'azi'), split_axis=0, concat_axis=0, til...  13.6 us
    all_to_all x2, starting transfers between devices, per_device(): adv = lax.all_to_all(adv, 'azi', split_axis=1, concat_axis=1, tiled=True)  12.8 us
    reshape x4, local copies, waits for them, and re-layouts, per_device(): adv.reshape(nrad, part, fields, halves, cells).transpose(0, 3, 1, 2, 4)  11 us
  transfers between devices with their start and end apart: 6, of which 6 were waited for; matrix products, arithmetic and copies ran while one was open for 20% of the time, Pallas kernels for 8%

profile of v3, /device:TPU:16, one launch (start us, length us, event | category | flops | bytes accessed | tf_op | source)
XLA Modules:
  0.0 248.7 jit_solution(507929416590633106)
XLA Ops:
  0.0 0.0 copy-start
  0.0 0.7 convert_bitcast_fusion
  0.7 0.7 maximum_bitcast_fusion
  1.4 19.2 %all-gather = f32[8,8,2]{1,2,0:T(2,128)S(1)} all-gather(f32[1,8,2]{1,2,0:T(2,128)S(1)} %maximum_bitcast_fusion), channel_id=1, replica_groups=mesh['rad'=8,'azi'=16] {'rad'}, dimensions={0}, use_global_device_ids=true | all-gather | bytes 576 | tf_op jit(solution)/shard_map/all_gather | solution.py:65
  20.6 0.1 reshape.111
  20.7 0.1 iota_add_fusion
  20.8 0.1 add.73
  20.9 1.2 gather_fusion
  22.1 1.2 gather_fusion.1
  23.3 4.0 %fusion.30 = (f32[8,8,8,1024]{3,2,1,0:T(8,128)}, f32[8,8,8,1024]{3,2,1,0:T(8,128)S(1)}) fusion(f32[8,8,16,1024]{3,2,1,0:T(8,128)} %param.5), kind=kLoop, calls=%fused_computation.39 | loop fusion | bytes 8388608 | tf_op jit(solution)/shard_map/slice | solution.py:74
  27.3 2.7 %copy.23 = f32[2,4,8,8,1024]{4,1,0,2,3:T(4,128)} copy(f32[2,4,8,8,1024]{4,3,2,1,0:T(8,128)S(1)} %bitcast.84) | data formatting | bytes 4194304 | tf_op jit(solution)/shard_map/reshape | solution.py:75
  30.0 7.4 %all-to-all-start = ((f32[128,4,1024]{2,1,0:T(4,128)}), f32[128,4,1024]{2,1,0:T(4,128)S(1)}, u32[]{:S(2)}, u32[]{:S(2)}) async-start(f32[128,4,1024]{2,1,0:T(4,128)} %bitcast.79), calls=%async_computation | async-start | bytes 4194304 | tf_op jit(solution)/shard_map/all_to_all | solution.py:80
  37.4 4.3 %copy.31 = f32[2,4,8,8,1024]{4,1,0,2,3:T(4,128)} copy(f32[2,4,8,8,1024]{4,3,2,1,0:T(8,128)} %bitcast.82) | data formatting | bytes 4194304 | tf_op jit(solution)/shard_map/reshape | solution.py:75
  41.7 24.4 %all-to-all-done = f32[128,4,1024]{2,1,0:T(4,128)S(1)} async-done(((f32[128,4,1024]{2,1,0:T(4,128)}), f32[128,4,1024]{2,1,0:T(4,128)S(1)}, u32[]{:S(2)}, u32[]{:S(2)}) %all-to-all-start) | async-done | bytes 2097184 | tf_op jit(solution)/shard_map/all_to_all | solution.py:80
  66.1 1.3 copy-done.2
  67.4 6.2 %all-to-all-start.3 = ((f32[128,4,1024]{2,1,0:T(4,128)}), f32[128,4,1024]{2,1,0:T(4,128)S(1)}, u32[]{:S(2)}, u32[]{:S(2)}) async-start(f32[128,4,1024]{2,1,0:T(4,128)} %bitcast.78), calls=%async_computation.3 | async-start | bytes 4194304 | tf_op jit(solution)/shard_map/all_to_all | solution.py:80
  73.6 2.8 %copy.24 = f32[128,4,1024]{2,0,1:T(8,128)S(1)} copy(f32[128,4,1024]{2,1,0:T(4,128)} %copy-done.2) | data formatting | bytes 4194304 | tf_op jit(solution)/shard_map/all_to_all | solution.py:80
  76.4 1.5 copy.25
  77.9 9.4 %shard_map.55 = f32[32,16,1024]{2,1,0:T(8,128)} custom-call(s32[32]{0:T(128)} %gather_fusion, f32[32]{0:T(128)} %gather_fusion.1, f32[32,16,1024]{2,1,0:T(8,128)} %bitcast.76), custom_call_target="tpu_custom_call" | custom-call | flops 15728640 | bytes 4194304 | tf_op jit(solution)/shard_map/pallas_call | solution.py:42
  87.2 4.2 %copy.26 = f32[32,16,1024]{2,0,1:T(8,128)} copy(f32[32,16,1024]{2,1,0:T(8,128)} %shard_map.55) | data formatting | bytes 4194304 | tf_op jit(solution)/shard_map/pallas_call | solution.py:42
  91.4 10.9 %all-to-all-done.3 = f32[128,4,1024]{2,1,0:T(4,128)S(1)} async-done(((f32[128,4,1024]{2,1,0:T(4,128)}), f32[128,4,1024]{2,1,0:T(4,128)S(1)}, u32[]{:S(2)}, u32[]{:S(2)}) %all-to-all-start.3) | async-done | bytes 2097184 | tf_op jit(solution)/shard_map/all_to_all | solution.py:80
  102.3 1.3 copy-done.1
  103.6 6.1 %all-to-all-start.1 = ((f32[32,16,1024]{2,0,1:T(8,128)}), f32[32,16,1024]{2,0,1:T(8,128)S(1)}, u32[]{:S(2)}, u32[]{:S(2)}) async-start(f32[32,16,1024]{2,0,1:T(8,128)} %copy.26), calls=%async_computation.1 | async-start | bytes 4194304 | tf_op jit(solution)/shard_map/all_to_all | solution.py:83
  109.7 2.8 %copy.32 = f32[128,4,1024]{2,0,1:T(8,128)S(1)} copy(f32[128,4,1024]{2,1,0:T(4,128)} %copy-done.1) | data formatting | bytes 4194304 | tf_op jit(solution)/shard_map/all_to_all | solution.py:80
  112.5 1.5 copy.33
  114.0 9.4 %shard_map.56 = f32[32,16,1024]{2,1,0:T(8,128)} custom-call(s32[32]{0:T(128)} %gather_fusion, f32[32]{0:T(128)} %gather_fusion.1, f32[32,16,1024]{2,1,0:T(8,128)} %bitcast.75), custom_call_target="tpu_custom_call" | custom-call | flops 15728640 | bytes 4194304 | tf_op jit(solution)/shard_map/pallas_call | solution.py:42
  123.4 4.1 %copy.34 = f32[32,16,1024]{2,0,1:T(8,128)} copy(f32[32,16,1024]{2,1,0:T(8,128)} %shard_map.56) | data formatting | bytes 4194304 | tf_op jit(solution)/shard_map/pallas_call | solution.py:42
  127.5 9.4 %all-to-all-done.1 = f32[32,16,1024]{2,0,1:T(8,128)S(1)} async-done(((f32[32,16,1024]{2,0,1:T(8,128)}), f32[32,16,1024]{2,0,1:T(8,128)S(1)}, u32[]{:S(2)}, u32[]{:S(2)}) %all-to-all-start.1) | async-done | bytes 2097184 | tf_op jit(solution)/shard_map/all_to_all | solution.py:83
  136.9 6.7 %all-to-all-start.4 = ((f32[32,16,1024]{2,0,1:T(8,128)}), f32[32,16,1024]{2,0,1:T(8,128)}, u32[]{:S(2)}, u32[]{:S(2)}) async-start(f32[32,16,1024]{2,0,1:T(8,128)} %copy.34), calls=%async_computation.4 | async-start | bytes 4194304 | tf_op jit(solution)/shard_map/all_to_all | solution.py:83
  143.6 1.6 reshape.84
  145.3 3.2 %copy.27 = f32[8,4,8,2,1024]{4,2,1,3,0:T(8,128)S(1)} copy(f32[8,4,8,2,1024]{4,1,0,3,2:T(4,128)} %reshape.84) | data formatting | bytes 4194304 | tf_op jit(solution)/shard_map/reshape | solution.py:84
  148.5 2.4 bitcast_add_fusion.1
  150.9 0.0 copy-done
  150.9 3.3 %fusion.18 = f32[64,8,1,1024]{3,0,1,2:T(8,128)S(1)} fusion(f32[8,64,64]{2,1,0:T(8,128)S(1)} %copy-done, f32[64,8,1024]{2,1,0:T(8,128)S(1)} %bitcast_add_fusion.1), kind=kOutput, calls=%fused_computation.21 | convolution fusion | flops 402653184 | bytes 4325376 | tf_op jit(solution)/shard_map/frk,kfj->rfj/dot_general | solution.py:89
  154.2 2.5 %copy.29 = f32[64,8,1,1024]{3,1,2,0:T(8,128)} copy(f32[64,8,1,1024]{3,0,1,2:T(8,128)S(1)} %fusion.18) | data formatting | bytes 4194304 | tf_op jit(solution)/shard_map/reshape | solution.py:90
  156.7 14.1 %all-to-all-done.4 = f32[32,16,1024]{2,0,1:T(8,128)} async-done(((f32[32,16,1024]{2,0,1:T(8,128)}), f32[32,16,1024]{2,0,1:T(8,128)}, u32[]{:S(2)}, u32[]{:S(2)}) %all-to-all-start.4) | async-done | bytes 2097184 | tf_op jit(solution)/shard_map/all_to_all | solution.py:83
  170.8 3.8 %all-to-all-start.2 = ((f32[64,8,1,1024]{3,1,2,0:T(8,128)}), f32[64,8,1,1024]{3,1,2,0:T(8,128)S(1)}, u32[]{:S(2)}, u32[]{:S(2)}) async-start(f32[64,8,1,1024]{3,1,2,0:T(8,128)} %copy.29), calls=%async_computation.2 | async-start | bytes 4194304 | tf_op jit(solution)/shard_map/all_to_all | solution.py:91
  174.7 2.8 %reshape.91 = f32[8,4,8,2,1024]{4,1,0,3,2:T(4,128)} reshape(f32[32,16,1024]{2,0,1:T(8,128)} %all-to-all-done.4) | data formatting | bytes 4194304 | tf_op jit(solution)/shard_map/reshape | solution.py:84
  177.5 3.2 %copy.35 = f32[8,4,8,2,1024]{4,2,1,3,0:T(8,128)S(1)} copy(f32[8,4,8,2,1024]{4,1,0,3,2:T(4,128)} %reshape.91) | data formatting | bytes 4194304 | tf_op jit(solution)/shard_map/reshape | solution.py:84
  180.7 2.4 bitcast_add_fusion
  183.1 3.3 %fusion.21 = f32[64,8,1,1024]{3,0,1,2:T(8,128)S(1)} fusion(f32[8,64,64]{2,1,0:T(8,128)S(1)} %copy-done, f32[64,8,1024]{2,1,0:T(8,128)S(1)} %bitcast_add_fusion), kind=kOutput, calls=%fused_computation.22 | convolution fusion | flops 402653184 | bytes 4325376 | tf_op jit(solution)/shard_map/frk,kfj->rfj/dot_general | solution.py:89
  186.4 2.5 %copy.37 = f32[64,8,1,1024]{3,1,2,0:T(8,128)} copy(f32[64,8,1,1024]{3,0,1,2:T(8,128)S(1)} %fusion.21) | data formatting | bytes 4194304 | tf_op jit(solution)/shard_map/reshape | solution.py:90
  188.9 18.2 %all-to-all-done.2 = f32[64,8,1,1024]{3,1,2,0:T(8,128)S(1)} async-done(((f32[64,8,1,1024]{3,1,2,0:T(8,128)}), f32[64,8,1,1024]{3,1,2,0:T(8,128)S(1)}, u32[]{:S(2)}, u32[]{:S(2)}) %all-to-all-start.2) | async-done | bytes 2097184 | tf_op jit(solution)/shard_map/all_to_all | solution.py:91
  207.2 4.3 %all-to-all-start.5 = ((f32[64,8,1,1024]{3,1,2,0:T(8,128)}), f32[64,8,1,1024]{3,1,2,0:T(8,128)}, u32[]{:S(2)}, u32[]{:S(2)}) async-start(f32[64,8,1,1024]{3,1,2,0:T(8,128)} %copy.37), calls=%async_computation.5 | async-start | bytes 4194304 | tf_op jit(solution)/shard_map/all_to_all | solution.py:91
  211.5 2.5 %copy.50 = f32[8,8,8,1,1024]{4,0,2,1,3:T(8,128)} copy(f32[8,8,8,1,1024]{4,2,1,0,3:T(8,128)S(1)} %bitcast.77) | data formatting | bytes 4194304 | tf_op jit(solution)/shard_map/all_to_all | solution.py:91
  214.0 29.4 %all-to-all-done.5 = f32[64,8,1,1024]{3,1,2,0:T(8,128)} async-done(((f32[64,8,1,1024]{3,1,2,0:T(8,128)}), f32[64,8,1,1024]{3,1,2,0:T(8,128)}, u32[]{:S(2)}, u32[]{:S(2)}) %all-to-all-start.5) | async-done | bytes 2097184 | tf_op jit(solution)/shard_map/all_to_all | solution.py:91
  243.5 2.9 %copy.49 = f32[8,8,8,1,1024]{4,0,2,1,3:T(8,128)S(1)} copy(f32[8,8,8,1,1024]{4,2,1,0,3:T(8,128)} %bitcast.36) | data formatting | bytes 4194304 | tf_op jit(solution)/shard_map/all_to_all | solution.py:91
  246.4 2.3 pad_maximum_fusion
  (12 shorter events, 0.0 us)
Async XLA Ops:
  0.0 150.9 %copy-start = (f32[8,64,64]{2,1,0:T(8,128)S(1)}, f32[8,64,64]{2,1,0:T(8,128)}, u32[]{:S(2)}) copy-start(f32[8,64,64]{2,1,0:T(8,128)} %param.9) | copy-start | bytes 393220
  30.0 36.1 %all-to-all-start = ((f32[128,4,1024]{2,1,0:T(4,128)}), f32[128,4,1024]{2,1,0:T(4,128)S(1)}, u32[]{:S(2)}, u32[]{:S(2)}) async-start(f32[128,4,1024]{2,1,0:T(4,128)} %bitcast.79), calls=%async_computation | async-start | bytes 4194304 | tf_op jit(solution)/shard_map/all_to_all | solution.py:80
  66.1 1.3 copy-start.2
  67.4 34.9 %all-to-all-start.3 = ((f32[128,4,1024]{2,1,0:T(4,128)}), f32[128,4,1024]{2,1,0:T(4,128)S(1)}, u32[]{:S(2)}, u32[]{:S(2)}) async-start(f32[128,4,1024]{2,1,0:T(4,128)} %bitcast.78), calls=%async_computation.3 | async-start | bytes 4194304 | tf_op jit(solution)/shard_map/all_to_all | solution.py:80
  102.3 1.3 copy-start.1
  103.6 33.3 %all-to-all-start.1 = ((f32[32,16,1024]{2,0,1:T(8,128)}), f32[32,16,1024]{2,0,1:T(8,128)S(1)}, u32[]{:S(2)}, u32[]{:S(2)}) async-start(f32[32,16,1024]{2,0,1:T(8,128)} %copy.26), calls=%async_computation.1 | async-start | bytes 4194304 | tf_op jit(solution)/shard_map/all_to_all | solution.py:83
  136.9 33.9 %all-to-all-start.4 = ((f32[32,16,1024]{2,0,1:T(8,128)}), f32[32,16,1024]{2,0,1:T(8,128)}, u32[]{:S(2)}, u32[]{:S(2)}) async-start(f32[32,16,1024]{2,0,1:T(8,128)} %copy.34), calls=%async_computation.4 | async-start | bytes 4194304 | tf_op jit(solution)/shard_map/all_to_all | solution.py:83
  145.3 3.2 %copy-start.4 = (f32[8,8]{1,0:T(8,128)S(1)}, f32[8,8]{1,0:T(8,128)}, u32[]{:S(2)}) copy-start(f32[8,8]{1,0:T(8,128)} %param.8) | copy-start | bytes 772
  170.8 36.3 %all-to-all-start.2 = ((f32[64,8,1,1024]{3,1,2,0:T(8,128)}), f32[64,8,1,1024]{3,1,2,0:T(8,128)S(1)}, u32[]{:S(2)}, u32[]{:S(2)}) async-start(f32[64,8,1,1024]{3,1,2,0:T(8,128)} %copy.29), calls=%async_computation.2 | async-start | bytes 4194304 | tf_op jit(solution)/shard_map/all_to_all | solution.py:91
  207.2 36.3 %all-to-all-start.5 = ((f32[64,8,1,1024]{3,1,2,0:T(8,128)}), f32[64,8,1,1024]{3,1,2,0:T(8,128)}, u32[]{:S(2)}, u32[]{:S(2)}) async-start(f32[64,8,1,1024]{3,1,2,0:T(8,128)} %copy.37), calls=%async_computation.5 | async-start | bytes 4194304 | tf_op jit(solution)/shard_map/all_to_all | solution.py:91
  243.5 2.9 %copy-start.3 = (f32[8,8,8,1,1024]{4,0,2,1,3:T(8,128)S(1)}, f32[8,8,8,1,1024]{4,0,2,1,3:T(8,128)}, u32[]{:S(2)}) copy-start(f32[8,8,8,1,1024]{4,0,2,1,3:T(8,128)} %copy.50) | copy-start | bytes 6291460

commit v4 on v3

--- a/solution.py
+++ b/solution.py
@@ -62,13 +62,19 @@
     pc = nrad
     chunks = planes // pc
     table = jnp.stack([orbit_shift.astype(jnp.float32), residual_speed])
-    table = lax.all_gather(table, "rad", axis=1, tiled=True)
-    shift_all = jnp.mod(table[0].astype(jnp.int32), nphi)
-    speed_all = table[1]
+    got = table[None]
+    step = 1
+    while step < nrad:
+        got = jnp.concatenate(
+            [got, lax.ppermute(got, "rad", [(i, (i + step) % nrad) for i in range(nrad)])]
+        )
+        step *= 2
+    me = lax.axis_index("rad")
+    table = got[jnp.mod(me - jnp.arange(nrad), nrad)]
     h = lax.axis_index("azi") % halves
-    order = (jnp.arange(nrad)[:, None] * rows + h * part + jnp.arange(part)[None, :]).reshape(-1)
-    shift = shift_all[order]
-    speed = speed_all[order]
+    table = lax.dynamic_slice_in_dim(table, h * part, part, axis=2).transpose(1, 0, 2).reshape(2, nrad * part)
+    shift = jnp.mod(table[0].astype(jnp.int32), nphi)
+    speed = table[1]
     sends = []
     for c in range(chunks):
         xc = fluid_state[:, :, c * pc:(c + 1) * pc, :]

time: 250 us -> 240 us (0.960)
  blocking collectives: 19.2 us -> 0 us
  starting transfers between devices: 34.5 us -> 42.8 us
  waiting for transfers between devices: 107 us -> 114 us
  local copies, waits for them, and re-layouts: 54.5 us -> 49.1 us
    ppermute x0 -> x3, waiting for transfers between devices: none -> 30.4 us  [per_device(): lax.ppermute(got, 'rad', [(i, (i + step) % nrad) for i in range(nrad)])]
    all_to_all x2, waiting for transfers between devices: 35.3 us -> 12.2 us  [per_device(): lax.all_to_all(sends[c], ('rad', 'azi'), split_axis=0, concat_axis=0, til...]
    all_gather x1 -> x0, blocking collectives: 19.2 us -> none  [per_device(): table = lax.all_gather(table, 'rad', axis=1, tiled=True)]
    all_to_all x2, starting transfers between devices: 13.6 us -> 19.8 us  [per_device(): lax.all_to_all(sends[c], ('rad', 'azi'), split_axis=0, concat_axis=0, til...]
    unnamed x11 -> x10, local copies, waits for them, and re-layouts: 2.73 us -> 0.02 us
  transfers between devices with their start and end apart: 6 -> 9, of which waited for: 6 -> 8; matrix products, arithmetic and copies ran while one was open for 20% -> 21% of each run, Pallas kernels for 8% -> 8%
where the time goes in v4:
time: 240 us; the launch traced here: 239 us
  waiting for transfers between devices  114 us (48%)
  local copies, waits for them, and re-layouts  49.1 us (20%)
  starting transfers between devices  42.8 us (18%)
  Pallas kernels  18.7 us (8%)
  matrix products  11.3 us (5%)
  other arithmetic  2.93 us (1%)
    all_to_all x2, waiting for transfers between devices, per_device(): lax.all_to_all(advanced, 'rad', split_axis=0, concat_axis=2, tiled=True)  47.7 us
    ppermute x3, waiting for transfers between devices, per_device(): lax.ppermute(got, 'rad', [(i, (i + step) % nrad) for i in range(nrad)])  30.4 us
    all_to_all x2, waiting for transfers between devices, per_device(): adv = lax.all_to_all(adv, 'azi', split_axis=1, concat_axis=1, tiled=True)  23.6 us
    all_to_all x2, starting transfers between devices, per_device(): lax.all_to_all(sends[c], ('rad', 'azi'), split_axis=0, concat_axis=0, til...  19.8 us
    pallas_call x2, Pallas kernels, remap_advect(): pl.pallas_call(remap_advect_kernel, out_shape=jax.ShapeDtypeStruct(rows_a...  18.7 us
    all_to_all x2, starting transfers between devices, per_device(): adv = lax.all_to_all(adv, 'azi', split_axis=1, concat_axis=1, tiled=True)  13 us
    all_to_all x2, waiting for transfers between devices, per_device(): lax.all_to_all(sends[c], ('rad', 'azi'), split_axis=0, concat_axis=0, til...  12.2 us
    reshape x4, local copies, waits for them, and re-layouts, per_device(): adv.reshape(nrad, part, fields, halves, cells).transpose(0, 3, 1, 2, 4)  11 us
  transfers between devices with their start and end apart: 9, of which 8 were waited for; matrix products, arithmetic and copies ran while one was open for 21% of the time, Pallas kernels for 8%

profile of v4, /device:TPU:16, one launch (start us, length us, event | category | flops | bytes accessed | tf_op | source)
XLA Modules:
  0.0 238.8 jit_solution(2889463672260775172)
XLA Ops:
  0.0 4.0 %fusion.32 = (f32[8,8,8,1024]{3,2,1,0:T(8,128)S(1)}, f32[8,8,8,1024]{3,2,1,0:T(8,128)}) fusion(f32[8,8,16,1024]{3,2,1,0:T(8,128)} %param.5), kind=kLoop, calls=%fused_computation.46 | loop fusion | bytes 8388608 | tf_op jit(solution)/shard_map/slice | solution.py:80
  4.0 2.7 %copy.28 = f32[2,4,8,8,1024]{4,1,0,2,3:T(4,128)} copy(f32[2,4,8,8,1024]{4,3,2,1,0:T(8,128)S(1)} %bitcast.77) | data formatting | bytes 4194304 | tf_op jit(solution)/shard_map/reshape | solution.py:81
  6.7 10.3 %all-to-all-start.3 = ((f32[128,4,1024]{2,1,0:T(4,128)}), f32[128,4,1024]{2,1,0:T(4,128)S(1)}, u32[]{:S(2)}, u32[]{:S(2)}) async-start(f32[128,4,1024]{2,1,0:T(4,128)} %bitcast.70), calls=%async_computation.3 | async-start | bytes 4194304 | tf_op jit(solution)/shard_map/all_to_all | solution.py:86
  17.1 0.0 copy-done.4
  17.1 1.8 collective-permute-start
  18.9 24.8 %collective-permute-done = f32[1,2,8]{2,1,0:T(2,128)S(1)} collective-permute-done((f32[1,2,8]{2,1,0:T(2,128)S(1)}, f32[1,2,8]{2,1,0:T(2,128)S(1)}, u32[]{:S(2)}, u32[]{:S(2)}) %collective-permute-start) | collective-permute-done | bytes 96 | tf_op jit(solution)/shard_map/ppermute | solution.py:69
  43.7 0.0 collective-permute-start.1
  43.7 4.8 %collective-permute-done.1 = f32[2,2,8]{2,1,0:T(2,128)S(1)} collective-permute-done((f32[2,2,8]{2,1,0:T(2,128)S(1)}, f32[2,2,8]{2,1,0:T(2,128)S(1)}, u32[]{:S(2)}, u32[]{:S(2)}) %collective-permute-start.1) | collective-permute-done | bytes 160 | tf_op jit(solution)/shard_map/ppermute | solution.py:69
  48.5 0.0 collective-permute-start.2
  48.5 4.3 %copy.20 = f32[2,4,8,8,1024]{4,1,0,2,3:T(4,128)} copy(f32[2,4,8,8,1024]{4,3,2,1,0:T(8,128)} %bitcast.75) | data formatting | bytes 4194304 | tf_op jit(solution)/shard_map/reshape | solution.py:81
  52.8 0.8 collective-permute-done.2
  53.7 0.6 gather_fusion
  54.2 0.1 dynamic-slice_bitcast_fusion
  54.3 0.1 convert_element_type.14
  54.4 0.7 squeeze.4.speed_ref
  55.1 0.5 and_select_fusion.shift_ref
  55.6 0.0 all-to-all-done.3
  55.6 9.5 %all-to-all-start = ((f32[128,4,1024]{2,1,0:T(4,128)}), f32[128,4,1024]{2,1,0:T(4,128)}, u32[]{:S(2)}, u32[]{:S(2)}) async-start(f32[128,4,1024]{2,1,0:T(4,128)} %bitcast.71), calls=%async_computation | async-start | bytes 4194304 | tf_op jit(solution)/shard_map/all_to_all | solution.py:86
  65.1 1.2 copy.29
  66.3 1.5 copy.30
  67.8 9.4 %shard_map.56 = f32[32,16,1024]{2,1,0:T(8,128)} custom-call(s32[32]{0:T(128)} %and_select_fusion.shift_ref, f32[32]{0:T(128)} %squeeze.4.speed_ref, f32[32,16,1024]{2,1,0:T(8,128)} %bitcast.69), custom_call_target="tpu_custom_call" | custom-call | flops 15728640 | bytes 4194304 | tf_op jit(solution)/shard_map/pallas_call | solution.py:42
  77.2 4.1 %copy.31 = f32[32,16,1024]{2,0,1:T(8,128)} copy(f32[32,16,1024]{2,1,0:T(8,128)} %shard_map.56) | data formatting | bytes 4194304 | tf_op jit(solution)/shard_map/pallas_call | solution.py:42
  81.3 12.2 %all-to-all-done = f32[128,4,1024]{2,1,0:T(4,128)} async-done(((f32[128,4,1024]{2,1,0:T(4,128)}), f32[128,4,1024]{2,1,0:T(4,128)}, u32[]{:S(2)}, u32[]{:S(2)}) %all-to-all-start) | async-done | bytes 2097184 | tf_op jit(solution)/shard_map/all_to_all | solution.py:86
  93.4 6.1 %all-to-all-start.4 = ((f32[32,16,1024]{2,0,1:T(8,128)}), f32[32,16,1024]{2,0,1:T(8,128)S(1)}, u32[]{:S(2)}, u32[]{:S(2)}) async-start(f32[32,16,1024]{2,0,1:T(8,128)} %copy.31), calls=%async_computation.4 | async-start | bytes 4194304 | tf_op jit(solution)/shard_map/all_to_all | solution.py:89
  99.6 2.8 %copy.21 = f32[128,4,1024]{2,0,1:T(8,128)S(1)} copy(f32[128,4,1024]{2,1,0:T(4,128)} %all-to-all-done) | data formatting | bytes 4194304 | tf_op jit(solution)/shard_map/all_to_all | solution.py:86
  102.4 1.5 copy.22
  103.8 9.4 %shard_map.55 = f32[32,16,1024]{2,1,0:T(8,128)} custom-call(s32[32]{0:T(128)} %and_select_fusion.shift_ref, f32[32]{0:T(128)} %squeeze.4.speed_ref, f32[32,16,1024]{2,1,0:T(8,128)} %bitcast.68), custom_call_target="tpu_custom_call" | custom-call | flops 15728640 | bytes 4194304 | tf_op jit(solution)/shard_map/pallas_call | solution.py:42
  113.2 4.1 %copy.23 = f32[32,16,1024]{2,0,1:T(8,128)} copy(f32[32,16,1024]{2,1,0:T(8,128)} %shard_map.55) | data formatting | bytes 4194304 | tf_op jit(solution)/shard_map/pallas_call | solution.py:42
  117.3 9.4 %all-to-all-done.4 = f32[32,16,1024]{2,0,1:T(8,128)S(1)} async-done(((f32[32,16,1024]{2,0,1:T(8,128)}), f32[32,16,1024]{2,0,1:T(8,128)S(1)}, u32[]{:S(2)}, u32[]{:S(2)}) %all-to-all-start.4) | async-done | bytes 2097184 | tf_op jit(solution)/shard_map/all_to_all | solution.py:89
  126.8 6.9 %all-to-all-start.1 = ((f32[32,16,1024]{2,0,1:T(8,128)}), f32[32,16,1024]{2,0,1:T(8,128)}, u32[]{:S(2)}, u32[]{:S(2)}) async-start(f32[32,16,1024]{2,0,1:T(8,128)} %copy.23), calls=%async_computation.1 | async-start | bytes 4194304 | tf_op jit(solution)/shard_map/all_to_all | solution.py:89
  133.6 1.6 reshape.108
  135.3 3.2 %copy.32 = f32[8,4,8,2,1024]{4,2,1,3,0:T(8,128)S(1)} copy(f32[8,4,8,2,1024]{4,1,0,3,2:T(4,128)} %reshape.108) | data formatting | bytes 4194304 | tf_op jit(solution)/shard_map/reshape | solution.py:90
  138.5 2.4 bitcast_add_fusion
  140.9 3.3 %fusion.21 = f32[64,8,1,1024]{3,0,1,2:T(8,128)S(1)} fusion(f32[8,64,64]{2,1,0:T(8,128)S(1)} %copy-done, f32[64,8,1024]{2,1,0:T(8,128)S(1)} %bitcast_add_fusion), kind=kOutput, calls=%fused_computation.21 | convolution fusion | flops 402653184 | bytes 4325376 | tf_op jit(solution)/shard_map/frk,kfj->rfj/dot_general | solution.py:95
  144.2 2.5 %copy.34 = f32[64,8,1,1024]{3,1,2,0:T(8,128)} copy(f32[64,8,1,1024]{3,0,1,2:T(8,128)S(1)} %fusion.21) | data formatting | bytes 4194304 | tf_op jit(solution)/shard_map/reshape | solution.py:96
  146.7 14.1 %all-to-all-done.1 = f32[32,16,1024]{2,0,1:T(8,128)} async-done(((f32[32,16,1024]{2,0,1:T(8,128)}), f32[32,16,1024]{2,0,1:T(8,128)}, u32[]{:S(2)}, u32[]{:S(2)}) %all-to-all-start.1) | async-done | bytes 2097184 | tf_op jit(solution)/shard_map/all_to_all | solution.py:89
  160.8 3.8 %all-to-all-start.5 = ((f32[64,8,1,1024]{3,1,2,0:T(8,128)}), f32[64,8,1,1024]{3,1,2,0:T(8,128)S(1)}, u32[]{:S(2)}, u32[]{:S(2)}) async-start(f32[64,8,1,1024]{3,1,2,0:T(8,128)} %copy.34), calls=%async_computation.5 | async-start | bytes 4194304 | tf_op jit(solution)/shard_map/all_to_all | solution.py:97
  164.7 2.9 %reshape.101 = f32[8,4,8,2,1024]{4,1,0,3,2:T(4,128)} reshape(f32[32,16,1024]{2,0,1:T(8,128)} %all-to-all-done.1) | data formatting | bytes 4194304 | tf_op jit(solution)/shard_map/reshape | solution.py:90
  167.5 3.2 %copy.24 = f32[8,4,8,2,1024]{4,2,1,3,0:T(8,128)S(1)} copy(f32[8,4,8,2,1024]{4,1,0,3,2:T(4,128)} %reshape.101) | data formatting | bytes 4194304 | tf_op jit(solution)/shard_map/reshape | solution.py:90
  170.8 2.4 bitcast_add_fusion.1
  173.1 3.3 %fusion.18 = f32[64,8,1,1024]{3,0,1,2:T(8,128)S(1)} fusion(f32[8,64,64]{2,1,0:T(8,128)S(1)} %copy-done, f32[64,8,1024]{2,1,0:T(8,128)S(1)} %bitcast_add_fusion.1), kind=kOutput, calls=%fused_computation.20 | convolution fusion | flops 402653184 | bytes 4325376 | tf_op jit(solution)/shard_map/frk,kfj->rfj/dot_general | solution.py:95
  176.4 2.5 %copy.26 = f32[64,8,1,1024]{3,1,2,0:T(8,128)} copy(f32[64,8,1,1024]{3,0,1,2:T(8,128)S(1)} %fusion.18) | data formatting | bytes 4194304 | tf_op jit(solution)/shard_map/reshape | solution.py:96
  178.9 18.2 %all-to-all-done.5 = f32[64,8,1,1024]{3,1,2,0:T(8,128)S(1)} async-done(((f32[64,8,1,1024]{3,1,2,0:T(8,128)}), f32[64,8,1,1024]{3,1,2,0:T(8,128)S(1)}, u32[]{:S(2)}, u32[]{:S(2)}) %all-to-all-start.5) | async-done | bytes 2097184 | tf_op jit(solution)/shard_map/all_to_all | solution.py:97
  197.2 4.3 %all-to-all-start.2 = ((f32[64,8,1,1024]{3,1,2,0:T(8,128)}), f32[64,8,1,1024]{3,1,2,0:T(8,128)}, u32[]{:S(2)}, u32[]{:S(2)}) async-start(f32[64,8,1,1024]{3,1,2,0:T(8,128)} %copy.26), calls=%async_computation.2 | async-start | bytes 4194304 | tf_op jit(solution)/shard_map/all_to_all | solution.py:97
  201.5 2.5 %copy.46 = f32[8,8,8,1,1024]{4,0,2,1,3:T(8,128)} copy(f32[8,8,8,1,1024]{4,2,1,0,3:T(8,128)S(1)} %bitcast.72) | data formatting | bytes 4194304 | tf_op jit(solution)/shard_map/all_to_all | solution.py:97
  204.0 29.4 %all-to-all-done.2 = f32[64,8,1,1024]{3,1,2,0:T(8,128)} async-done(((f32[64,8,1,1024]{3,1,2,0:T(8,128)}), f32[64,8,1,1024]{3,1,2,0:T(8,128)}, u32[]{:S(2)}, u32[]{:S(2)}) %all-to-all-start.2) | async-done | bytes 2097184 | tf_op jit(solution)/shard_map/all_to_all | solution.py:97
  233.5 2.9 %copy.47 = f32[8,8,8,1,1024]{4,0,2,1,3:T(8,128)S(1)} copy(f32[8,8,8,1,1024]{4,2,1,0,3:T(8,128)} %bitcast.18) | data formatting | bytes 4194304 | tf_op jit(solution)/shard_map/all_to_all | solution.py:97
  236.4 2.3 pad_maximum_fusion
  (18 shorter events, 0.1 us)
Async XLA Ops:
  0.0 140.9 %copy-start = (f32[8,64,64]{2,1,0:T(8,128)S(1)}, f32[8,64,64]{2,1,0:T(8,128)}, u32[]{:S(2)}) copy-start(f32[8,64,64]{2,1,0:T(8,128)} %param.9) | copy-start | bytes 393220
  6.7 10.3 %copy-start.4 = (s32[8]{0:T(128)S(1)}, s32[8]{0:T(128)}, u32[]{:S(2)}) copy-start(s32[8]{0:T(128)} %param.6) | copy-start | bytes 100
  6.7 10.4 %copy-start.3 = (f32[8]{0:T(128)S(1)}, f32[8]{0:T(128)}, u32[]{:S(2)}) copy-start(f32[8]{0:T(128)} %param.7) | copy-start | bytes 100
  6.7 48.9 %all-to-all-start.3 = ((f32[128,4,1024]{2,1,0:T(4,128)}), f32[128,4,1024]{2,1,0:T(4,128)S(1)}, u32[]{:S(2)}, u32[]{:S(2)}) async-start(f32[128,4,1024]{2,1,0:T(4,128)} %bitcast.70), calls=%async_computation.3 | async-start | bytes 4194304 | tf_op jit(solution)/shard_map/all_to_all | solution.py:86
  17.1 26.6 %collective-permute-start = (f32[1,2,8]{2,1,0:T(2,128)S(1)}, f32[1,2,8]{2,1,0:T(2,128)S(1)}, u32[]{:S(2)}, u32[]{:S(2)}) collective-permute-start(f32[1,2,8]{2,1,0:T(2,128)S(1)} %maximum_bitcast_fusion), channel_id=1, source_target_pairs={{0,16},{16,32},{32,48},{48,64},{64,80},{80,96},{96,112},{112,0},{1... | collective-permute-start | bytes 200 | tf_op jit(solution)/shard_map/ppermute | solution.py:69
  43.7 4.8 %collective-permute-start.1 = (f32[2,2,8]{2,1,0:T(2,128)S(1)}, f32[2,2,8]{2,1,0:T(2,128)S(1)}, u32[]{:S(2)}, u32[]{:S(2)}) collective-permute-start(f32[2,2,8]{2,1,0:T(2,128)S(1)} %pad_maximum_fusion.3), channel_id=1, source_target_pairs={{0,32},{16,48},{32,64},{48,80},{64,96},{80,112},{96,0},{112,16},{1... | collective-permute-start | bytes 392 | tf_op jit(solution)/shard_map/ppermute | solution.py:69
  48.5 5.1 %collective-permute-start.2 = (f32[4,2,8]{2,1,0:T(2,128)S(1)}, f32[4,2,8]{2,1,0:T(2,128)S(1)}, u32[]{:S(2)}, u32[]{:S(2)}) collective-permute-start(f32[4,2,8]{2,1,0:T(2,128)S(1)} %pad_maximum_fusion.2), channel_id=1, source_target_pairs={{0,64},{16,80},{32,96},{48,112},{64,0},{80,16},{96,32},{112,48},{1... | collective-permute-start | bytes 776 | tf_op jit(solution)/shard_map/ppermute | solution.py:69
  55.6 37.8 %all-to-all-start = ((f32[128,4,1024]{2,1,0:T(4,128)}), f32[128,4,1024]{2,1,0:T(4,128)}, u32[]{:S(2)}, u32[]{:S(2)}) async-start(f32[128,4,1024]{2,1,0:T(4,128)} %bitcast.71), calls=%async_computation | async-start | bytes 4194304 | tf_op jit(solution)/shard_map/all_to_all | solution.py:86
  93.4 33.3 %all-to-all-start.4 = ((f32[32,16,1024]{2,0,1:T(8,128)}), f32[32,16,1024]{2,0,1:T(8,128)S(1)}, u32[]{:S(2)}, u32[]{:S(2)}) async-start(f32[32,16,1024]{2,0,1:T(8,128)} %copy.31), calls=%async_computation.4 | async-start | bytes 4194304 | tf_op jit(solution)/shard_map/all_to_all | solution.py:89
  126.8 34.1 %all-to-all-start.1 = ((f32[32,16,1024]{2,0,1:T(8,128)}), f32[32,16,1024]{2,0,1:T(8,128)}, u32[]{:S(2)}, u32[]{:S(2)}) async-start(f32[32,16,1024]{2,0,1:T(8,128)} %copy.23), calls=%async_computation.1 | async-start | bytes 4194304 | tf_op jit(solution)/shard_map/all_to_all | solution.py:89
  135.3 3.2 %copy-start.2 = (f32[8,8]{1,0:T(8,128)S(1)}, f32[8,8]{1,0:T(8,128)}, u32[]{:S(2)}) copy-start(f32[8,8]{1,0:T(8,128)} %param.8) | copy-start | bytes 772
  160.8 36.3 %all-to-all-start.5 = ((f32[64,8,1,1024]{3,1,2,0:T(8,128)}), f32[64,8,1,1024]{3,1,2,0:T(8,128)S(1)}, u32[]{:S(2)}, u32[]{:S(2)}) async-start(f32[64,8,1,1024]{3,1,2,0:T(8,128)} %copy.34), calls=%async_computation.5 | async-start | bytes 4194304 | tf_op jit(solution)/shard_map/all_to_all | solution.py:97
  197.2 36.3 %all-to-all-start.2 = ((f32[64,8,1,1024]{3,1,2,0:T(8,128)}), f32[64,8,1,1024]{3,1,2,0:T(8,128)}, u32[]{:S(2)}, u32[]{:S(2)}) async-start(f32[64,8,1,1024]{3,1,2,0:T(8,128)} %copy.26), calls=%async_computation.2 | async-start | bytes 4194304 | tf_op jit(solution)/shard_map/all_to_all | solution.py:97
  233.5 2.9 %copy-start.1 = (f32[8,8,8,1,1024]{4,0,2,1,3:T(8,128)S(1)}, f32[8,8,8,1,1024]{4,0,2,1,3:T(8,128)}, u32[]{:S(2)}) copy-start(f32[8,8,8,1,1024]{4,0,2,1,3:T(8,128)} %copy.46) | copy-start | bytes 6291460
